TPU v7x, 256 devices: a whole 4x4x8 slice. The times are simulated.
256 devices in a mesh: outer: 32 (over z, x), inner: 8 (over y, core).
Axes of the slice: x: 4, y: 4, z: 8, core: 2. Of those that a mesh axis runs over, the one named last changes fastest.
Arguments:
- queries: bfloat16 [262144, 1024], P(('outer', 'inner')), may hold values from -6 to 6
- keys: bfloat16 [262144, 1024], P(('outer', 'inner')), may hold values from -6 to 6
- values: bfloat16 [262144, 1024], P(('outer', 'inner')), may hold values from -6 to 6
- norm_gain: float32 [1024], replicated, may hold values from 0.1 to 1.9
- out_weight: bfloat16 [1024, 2048], replicated, may hold values from -0.1875 to 0.1875
Outputs:
- mixed: bfloat16 [262144, 2048], P(('outer', 'inner'))
All inputs are finite; a program needn't handle non-finite values.
Results may differ from a plain program's by a relative error of at most 0.0058.
Values sent between devices are 32-bit elements; how exact they have to be, the bound alone decides.
No kernel may reach another device: no remote copies, remote signals or barrier semaphores. Data moves between devices by JAX's collectives and lax.ppermute only.
A program may use at most 320 MiB of HBM per device.

v0:
```python
import jax
import jax.numpy as jnp
from jax import lax
from jax.sharding import PartitionSpec as P

H = 8
DH = 128
C = 128


def prefix(value, axis, join, neutral):
    count, mine = (lax.axis_size(axis), lax.axis_index(axis))
    pieces = lax.all_gather(value, axis)
    running = jnp.full_like(value, 0) + jnp.asarray(neutral, value.dtype)

    def step(position, running):
        longer = join(running, pieces[position])
        return jnp.where(position < mine, longer, running)

    return lax.fori_loop(0, count - 1, step, running)


def add_states(earlier, later):
    return earlier + later


def on_device(queries, keys, values, norm_gain, out_weight):
    tok_rows = queries.shape[0]
    blocks = tok_rows // C
    query_blocks = queries.reshape(blocks, C, H, DH)
    key_blocks = keys.reshape(blocks, C, H, DH)
    value_blocks = values.reshape(blocks, C, H, DH)
    states = jnp.einsum(
        "nchd,nche->nhde", key_blocks, value_blocks, preferred_element_type=jnp.float32
    )
    local_total = jnp.sum(states, axis=0)
    running = jnp.cumsum(states, axis=0)
    empty_state = jnp.zeros_like(local_total)
    within = jnp.concatenate([empty_state[None], running[:-1]], axis=0)
    scores = jnp.einsum(
        "nchd,nshd->nhcs", query_blocks, key_blocks, preferred_element_type=jnp.float32
    )
    causal = lax.broadcasted_iota(jnp.int32, (C, C), 0) >= lax.broadcasted_iota(
        jnp.int32, (C, C), 1
    )
    weights = jnp.where(causal[None, None], scores, 0.0).astype(jnp.bfloat16)
    inside = jnp.einsum(
        "nhcs,nshd->nchd", weights, value_blocks, preferred_element_type=jnp.float32
    )
    inner_part = prefix(local_total, "inner", add_states, empty_state)
    group_sum = lax.psum(local_total, "inner")
    outer_part = prefix(group_sum, "outer", add_states, empty_state)
    carried = outer_part + inner_part
    prefix_low = (carried[None] + within).astype(jnp.bfloat16)
    carried_term = jnp.einsum(
        "nchd,nhde->nche", query_blocks, prefix_low, preferred_element_type=jnp.float32
    )
    attended = inside + carried_term
    mean_square = jnp.mean(attended * attended, axis=-1, keepdims=True)
    normed = attended * lax.rsqrt(mean_square + 1e-06) * norm_gain.reshape(H, DH)
    normed = normed.astype(jnp.bfloat16).reshape(tok_rows, H * DH)
    return jnp.dot(normed, out_weight, preferred_element_type=jnp.float32).astype(jnp.bfloat16)


def solution(mesh):
    return jax.shard_map(
        on_device,
        mesh=mesh,
        in_specs=(
            P(("outer", "inner"), None),
            P(("outer", "inner"), None),
            P(("outer", "inner"), None),
            P(),
            P(),
        ),
        out_specs=P(("outer", "inner"), None),
        check_vma=False,
    )
```

profile of v0, /device:TPU:1, one launch (start us, length us, event | category | flops | bytes accessed | tf_op | source)
XLA Modules:
  0.0 331.9 jit_solution(8556878679005771452)
XLA Ops:
  6.5 3.5 %copy.27 = bf16[128,8,8,128]{3,2,1,0:T(8,128)(2,1)} copy(bf16[128,8,8,128]{3,1,2,0:T(8,128)(2,1)} %bitcast.39) | data formatting | bytes 4194304
  10.1 3.3 copy.20
  13.4 3.0 copy.28
  16.4 3.6 %fusion.13 = (f32[8,128,128]{2,1,0:T(8,128)}, f32[8,8,128,128]{3,2,1,0:T(8,128)}) fusion(bf16[8,128,8,128]{1,3,2,0:T(8,128)(2,1)S(1)} %copy.20, bf16[8,128,8,128]{3,2,1,0:T(8,128)(2,1)S(1)} %bitcast.35), kind=kOutput, calls=%fused_computation.21 | convolution fusion | flops 269352960 | bytes 8912896 | tf_op jit(solution)/shard_map/nchd,nche->nhde/dot_general | solution.py:33
  20.0 39.0 %all-gather.6.cloned.1.call-done = f32[64,128,128]{2,1,0:T(8,128)} async-done(((f32[8,128,128]{2,1,0:T(8,128)}), f32[64,128,128]{2,1,0:T(8,128)}) %all-gather.6.cloned.1.call-update) | async-done | bytes 4194320 | tf_op jit(solution)/shard_map/all_gather | solution.py:13
  59.7 66.1 %all-reduce.3.cloned.1.call-done = f32[1,8,128,128]{3,2,1,0:T(8,128)} async-done(((f32[1,8,128,128]{3,2,1,0:T(8,128)}), f32[1,8,128,128]{3,2,1,0:T(8,128)}) %all-reduce.3.cloned.1.call-update) | async-done | bytes 524304 | tf_op jit(solution)/shard_map/psum | solution.py:51
  125.8 2.4 copy.26
  128.7 3.8 %fusion.14 = f32[8,8,128,128]{3,2,1,0:T(8,128)S(1)} fusion(f32[8,8,128,128]{3,2,1,0:T(8,128)S(1)} %copy-done.2), kind=kOutput, calls=%fused_computation.22 | output fusion | flops 7340032 | bytes 8388608 | tf_op jit(solution)/shard_map/jit(cumsum)/reduce_window_sum | solution.py:37
  132.5 2.1 slice.4
  134.5 6.4 %fusion.3 = f32[8,8,128,128]{2,3,1,0:T(8,128)} fusion(bf16[8,128,8,128]{3,2,1,0:T(8,128)(2,1)} %bitcast.36, bf16[8,128,8,128]{1,3,2,0:T(8,128)(2,1)} %copy-done, pred[128,128]{1,0:T(8,128)(4,1)S(1)} %iota_compare_fusion, bf16[8,128,8,128]{3,2,1,0:T(8,128)(2,1)S(1)} %bitcast.33), kind=kOutput, calls=%fused_computation.11 | convolution fusion | flops 538968064 | bytes 10502144 | tf_op jit(solution)/shard_map/nhcs,nshd->nchd/dot_general | solution.py:47
  140.9 8.8 %while.29 = (s32[]{:T(128)}, f32[8,128,128]{2,1,0:T(8,128)S(1)}, s32[]{:T(128)}, f32[8,8,128,128]{3,2,1,0:T(8,128)}, s32[]{:T(128)}, /*index=5*/s32[]{:T(128)}) while((s32[]{:T(128)}, f32[8,128,128]{2,1,0:T(8,128)S(1)}, s32[]{:T(128)}, f32[8,8,128,128]{3,2,1,0:T(8,128)}, s32[]{:T(128)}, /*index=5*/s32[]{:T(128)}) %tuple.73), condition=%wide.region_5.6_spmd.clone, body=%wide.region_4.5_spmd.clone.sunk | while | flops 393220 | bytes 1572965 | solution.py:20
  140.9 1.3 add_select_fusion.5
  142.2 1.3 add_select_fusion.5
  143.5 1.2 add_select_fusion.5
  144.8 1.2 add_select_fusion.5
  146.0 1.2 add_select_fusion.5
  147.3 1.2 add_select_fusion.5
  148.5 1.2 add_select_fusion.5
  149.8 118.8 %all-gather.4.cloned.1.call-done = f32[32,8,128,128]{3,2,1,0:T(8,128)} async-done(((f32[1,8,128,128]{3,2,1,0:T(8,128)}), f32[32,8,128,128]{3,2,1,0:T(8,128)}) %all-gather.4.cloned.1.call-update) | async-done | bytes 16777232 | tf_op jit(solution)/shard_map/all_gather | solution.py:13
  268.6 38.8 %while.28 = (s32[]{:T(128)}, f32[8,128,128]{2,1,0:T(8,128)S(1)}, s32[]{:T(128)}, f32[32,8,128,128]{3,2,1,0:T(8,128)}, s32[]{:T(128)}, /*index=5*/s32[]{:T(128)}) while((s32[]{:T(128)}, f32[8,128,128]{2,1,0:T(8,128)S(1)}, s32[]{:T(128)}, f32[32,8,128,128]{3,2,1,0:T(8,128)}, s32[]{:T(128)}, /*index=5*/s32[]{:T(128)}) %tuple.61), condition=%wide.region_3.4_spmd.clone, body=%wide.region_2.3_spmd.clone.sunk | while | flops 393220 | bytes 1572965 | solution.py:20
  269.9 1.2 add_select_fusion.4
  271.1 1.2 add_select_fusion.4
  272.4 1.2 add_select_fusion.4
  273.6 1.2 add_select_fusion.4
  274.9 1.2 add_select_fusion.4
  276.1 1.2 add_select_fusion.4
  282.4 1.2 add_select_fusion.4
  296.1 1.2 add_select_fusion.4
  306.1 1.2 add_select_fusion.4
  307.5 4.9 %multiply_reduce_fusion = (f32[8,128,8]{1,2,0:T(8,128)S(1)}, f32[8,128,8,128]{1,3,2,0:T(8,128)S(1)}) fusion(bf16[8,128,8,128]{3,2,1,0:T(8,128)(2,1)S(1)} %bitcast.34, f32[7,8,128,128]{3,2,1,0:T(8,128)} %slice.4, f32[8,128,128]{2,1,0:T(8,128)S(1)} %add.85, f32[8,8,128,128]{2,3,1,0:T(8,128)} %fusion.3), kind=kOutput, calls=%fused_computation.4 | convolution fusion | flops 273670144 | bytes 14712832 | tf_op jit(solution)/shard_map/nchd,nhde->nche/dot_general | solution.py:55
  313.3 2.8 copy.24
  316.1 9.3 %convolution_convert_fusion = bf16[1024,2048]{1,0:T(8,128)(2,1)} fusion(bf16[1024,2048]{1,0:T(8,128)(2,1)} %param.13, bf16[128,8,8,128]{3,2,1,0:T(8,128)(2,1)} %bitcast.42), kind=kOutput, calls=%fused_computation.7 | convolution fusion | flops 4297064448 | bytes 10485760 | tf_op jit(solution)/shard_map/dot_general | solution.py:62
  (42 shorter events, 29.2 us)
Async XLA Ops:
  6.5 52.4 %all-gather.6.cloned.1.call-start = ((), (), s32[]{:S(2)}) async-start(), calls=%async_computation.2 | async-start | bytes 4718592 | tf_op jit(solution)/shard_map/all_gather | solution.py:13
  13.4 3.0 copy-start
  16.3 3.6 %copy-start.1 = (bf16[128,8,8,128]{3,2,1,0:T(8,128)(2,1)}, bf16[128,8,8,128]{3,2,1,0:T(8,128)(2,1)S(1)}, u32[]{:S(2)}) copy-start(bf16[128,8,8,128]{3,2,1,0:T(8,128)(2,1)S(1)} %copy.28) | copy-start | bytes 6291460
  58.9 66.9 %all-reduce.3.cloned.1.call-start = ((), (), s32[]{:S(2)}) async-start(), calls=%async_computation | async-start | bytes 1048576 | tf_op jit(solution)/shard_map/psum | solution.py:51
  59.7 208.9 %all-gather.4.cloned.1.call-start = ((), (), s32[]{:S(2)}) async-start(), calls=%async_computation.1 | async-start | bytes 17301504 | tf_op jit(solution)/shard_map/all_gather | solution.py:13
  125.8 2.8 copy-start.2
  307.4 5.0 %copy-start.3 = (f32[1024]{0:T(1024)S(1)}, f32[1024]{0:T(1024)}, u32[]{:S(2)}) copy-start(f32[1024]{0:T(1024)} %param.12) | copy-start | bytes 12292
Sparse Core Ops, SparseCore 0:
  20.1 38.8 all-gather.5
  62.1 63.6 all-reduce.2
  128.4 140.1 all-gather.3
where the time goes:
time: 334 us; the launch traced here: 332 us
  waiting for transfers between devices  225 us (67%)
  other arithmetic  51.4 us (15%)
  matrix products  24.2 us (7%)
  local copies, waits for them, and re-layouts  17.5 us (5%)
  between operations  13.3 us (4%)
    all_gather x2, waiting for transfers between devices, prefix(): pieces = lax.all_gather(value, axis)  158 us
    psum x1, waiting for transfers between devices, on_device(): group_sum = lax.psum(local_total, 'inner')  66.1 us
    select_n x38, other arithmetic, step(): return jnp.where(position < mine, longer, running)  46.7 us
    dot_general x1, matrix products, on_device(): jnp.dot(normed, out_weight, preferred_element_type=jnp.float32)  9.33 us
    unnamed x11, local copies, waits for them, and re-layouts  9.33 us
  transfers between devices with their start and end apart: 3, of which 3 were waited for; matrix products, arithmetic and copies ran while one was open for 7% of the time, Pallas kernels for 0%

commit v1 on v0

--- a/solution.py
+++ b/solution.py
@@ -8,20 +8,24 @@
 C = 128
 
 
-def prefix(value, axis, join, neutral):
-    count, mine = (lax.axis_size(axis), lax.axis_index(axis))
-    pieces = lax.all_gather(value, axis)
-    running = jnp.full_like(value, 0) + jnp.asarray(neutral, value.dtype)
-
-    def step(position, running):
-        longer = join(running, pieces[position])
-        return jnp.where(position < mine, longer, running)
-
-    return lax.fori_loop(0, count - 1, step, running)
+def exclusive_cumsum(rows):
+    running = jnp.cumsum(rows, axis=0)
+    return jnp.concatenate([jnp.zeros_like(rows[:1]), running[:-1]], axis=0), running[-1]
 
 
-def add_states(earlier, later):
-    return earlier + later
+def carried_state(local_total):
+    n_inner = lax.axis_size("inner")
+    n_outer = lax.axis_size("outer")
+    size = local_total.size
+    chunks = local_total.reshape(n_inner, size // n_inner)
+    gathered = lax.all_to_all(chunks, "inner", 0, 0, tiled=True)
+    inner_before, group_total = exclusive_cumsum(gathered)
+    pieces = lax.all_to_all(group_total.reshape(n_outer, -1), "outer", 0, 0, tiled=True)
+    outer_before, _ = exclusive_cumsum(pieces)
+    outer_chunk = lax.all_to_all(outer_before, "outer", 0, 0, tiled=True).reshape(-1)
+    summed = inner_before + outer_chunk[None, :]
+    back = lax.all_to_all(summed, "inner", 0, 0, tiled=True)
+    return back.reshape(local_total.shape)
 
 
 def on_device(queries, keys, values, norm_gain, out_weight):
@@ -47,10 +51,7 @@
     inside = jnp.einsum(
         "nhcs,nshd->nchd", weights, value_blocks, preferred_element_type=jnp.float32
     )
-    inner_part = prefix(local_total, "inner", add_states, empty_state)
-    group_sum = lax.psum(local_total, "inner")
-    outer_part = prefix(group_sum, "outer", add_states, empty_state)
-    carried = outer_part + inner_part
+    carried = carried_state(local_total)
     prefix_low = (carried[None] + within).astype(jnp.bfloat16)
     carried_term = jnp.einsum(
         "nchd,nhde->nche", query_blocks, prefix_low, preferred_element_type=jnp.float32

time: 334 us -> 97.8 us (0.29)
  waiting for transfers between devices: 225 us -> 4.86 us
  other arithmetic: 51.4 us -> 3.98 us
  blocking collectives: 0 us -> 34.7 us
  between operations: 13.3 us -> 0.11 us
  starting transfers between devices: 0.04 us -> 10.8 us
    all_gather x2 -> x0, waiting for transfers between devices: 158 us -> none  [prefix(): pieces = lax.all_gather(value, axis)]
    psum x1 -> x0, waiting for transfers between devices: 66.1 us -> none  [on_device(): group_sum = lax.psum(local_total, 'inner')]
    select_n x38 -> x0, other arithmetic: 46.7 us -> none  [step(): return jnp.where(position < mine, longer, running)]
    all_to_all x0 -> x2, blocking collectives: none -> 34.7 us  [the longest x1 19.7 us: carried_state(): lax.all_to_all(group_total.reshape(n_outer, -1), 'outer', 0, 0, tiled=True)]
    all_to_all x0 -> x2, starting transfers between devices: none -> 10.8 us  [the longest x1 6.97 us: carried_state(): back = lax.all_to_all(summed, 'inner', 0, 0, tiled=True)]
    all_to_all x0 -> x2, waiting for transfers between devices: none -> 4.86 us  [the longest x1 2.99 us: carried_state(): back = lax.all_to_all(summed, 'inner', 0, 0, tiled=True)]
  transfers between devices with their start and end apart: 3 -> 2, of which waited for: 3 -> 2; matrix products, arithmetic and copies ran while one was open for 7% -> 13% of each run, Pallas kernels for 0% -> 0%
where the time goes in v1:
time: 97.8 us; the launch traced here: 97.3 us
  blocking collectives  34.7 us (35%)
  matrix products  24 us (25%)
  local copies, waits for them, and re-layouts  18.7 us (19%)
  starting transfers between devices  10.8 us (11%)
  waiting for transfers between devices  4.86 us (5%)
  other arithmetic  3.98 us (4%)
    all_to_all x1, blocking collectives, carried_state(): lax.all_to_all(group_total.reshape(n_outer, -1), 'outer', 0, 0, tiled=True)  19.7 us
    all_to_all x1, blocking collectives, carried_state(): gathered = lax.all_to_all(chunks, 'inner', 0, 0, tiled=True)  15.1 us
    dot_general x1, matrix products, on_device(): jnp.dot(normed, out_weight, preferred_element_type=jnp.float32)  9.33 us
    unnamed x11, local copies, waits for them, and re-layouts  8.49 us
    all_to_all x1, starting transfers between devices, carried_state(): back = lax.all_to_all(summed, 'inner', 0, 0, tiled=True)  6.97 us
    dot_general x1, matrix products, on_device(): jnp.einsum('nhcs,nshd->nchd', weights, value_blocks, preferred_element_ty...  6.39 us
    dot_general x1, matrix products, on_device(): jnp.einsum('nchd,nhde->nche', query_blocks, prefix_low, preferred_element...  5.53 us
    all_to_all x1, starting transfers between devices, carried_state(): lax.all_to_all(outer_before, 'outer', 0, 0, tiled=True).reshape(-1)  3.84 us
  transfers between devices with their start and end apart: 2, of which 2 were waited for; matrix products, arithmetic and copies ran while one was open for 13% of the time, Pallas kernels for 0%

profile of v1, /device:TPU:1, one launch (start us, length us, event | category | flops | bytes accessed | tf_op | source)
XLA Modules:
  0.0 97.3 jit_solution(12036753795374327165)
XLA Ops:
  0.0 3.5 %copy.33 = bf16[128,8,8,128]{3,2,1,0:T(8,128)(2,1)} copy(bf16[128,8,8,128]{3,1,2,0:T(8,128)(2,1)} %bitcast.47) | data formatting | bytes 4194304
  3.5 3.3 %copy.20 = bf16[8,128,8,128]{1,3,2,0:T(8,128)(2,1)S(1)} copy(bf16[8,128,8,128]{3,2,1,0:T(8,128)(2,1)} %bitcast.43) | data formatting | bytes 4194304 | tf_op jit(solution)/shard_map/reshape | solution.py:35
  6.8 2.2 %copy.34 = bf16[128,8,8,128]{3,2,1,0:T(8,128)(2,1)S(1)} copy(bf16[128,8,8,128]{3,1,2,0:T(8,128)(2,1)} %bitcast.48) | data formatting | bytes 4194304
  9.0 0.0 copy-start
  9.0 2.8 %fusion.13 = (f32[8,128,128]{2,1,0:T(8,128)S(1)}, f32[8,8,128,128]{3,2,1,0:T(8,128)}) fusion(bf16[8,128,8,128]{1,3,2,0:T(8,128)(2,1)S(1)} %copy.20, bf16[8,128,8,128]{3,2,1,0:T(8,128)(2,1)S(1)} %bitcast.39), kind=kOutput, calls=%fused_computation.23 | convolution fusion | flops 269352960 | bytes 8912896 | tf_op jit(solution)/shard_map/nchd,nche->nhde/dot_general | solution.py:37
  11.8 0.0 copy-done
  11.8 15.1 %all_to_all.42 = f32[8,1,16384]{2,1,0:T(1,128)S(1)} all-to-all(f32[8,1,16384]{2,1,0:T(1,128)S(1)} %bitcast.46), channel_id=1, replica_groups=mesh['outer'=32,'inner'=8] {'inner'}, dimensions={0} | all-to-all | bytes 1048576 | tf_op jit(solution)/shard_map/all_to_all | solution.py:21
  26.9 0.3 copy.56
  27.2 0.5 reduce_window_sum.33
  27.7 0.1 slice.17
  27.7 19.7 %all_to_all.43 = f32[32,1,512]{2,1,0:T(1,128)S(1)} all-to-all(f32[32,1,512]{2,1,0:T(1,128)S(1)} %bitcast.55), channel_id=1, replica_groups=mesh['outer'=32,'inner'=8] {'outer'}, dimensions={0} | all-to-all | bytes 131072 | tf_op jit(solution)/shard_map/all_to_all | solution.py:23
  47.4 0.1 reduce_window_sum.34
  47.5 0.7 copy.24
  48.2 3.8 %all-to-all-start.2 = ((f32[32,1,512]{2,1,0:T(1,128)}), f32[32,1,512]{2,1,0:T(1,128)S(1)}, u32[]{:S(2)}, u32[]{:S(2)}) async-start(f32[32,1,512]{2,1,0:T(1,128)} %copy.24), calls=%async_computation.2 | async-start | bytes 131072 | tf_op jit(solution)/shard_map/all_to_all | solution.py:25
  52.0 2.5 %fusion.14 = f32[8,8,128,128]{3,2,1,0:T(8,128)S(1)} fusion(f32[8,8,128,128]{3,2,1,0:T(8,128)} %get-tuple-element.6), kind=kOutput, calls=%fused_computation.24 | output fusion | flops 7340032 | bytes 8388608 | tf_op jit(solution)/shard_map/jit(cumsum)/reduce_window_sum | solution.py:41
  54.6 0.0 copy-start.1
  54.6 2.0 %slice.19 = f32[7,8,128,128]{3,2,1,0:T(8,128)} slice(f32[8,8,128,128]{3,2,1,0:T(8,128)S(1)} %fusion.14), slice={[0:7], [0:8], [0:128], [0:128]} | slice | bytes 7340032 | tf_op jit(solution)/shard_map/slice | solution.py:43
  56.6 0.4 copy-done.1
  57.1 2.0 %copy.32 = bf16[128,8,8,128]{3,2,1,0:T(8,128)(2,1)} copy(bf16[128,8,8,128]{3,1,2,0:T(8,128)(2,1)S(1)} %bitcast.49) | data formatting | bytes 4194304
  59.0 1.9 %all-to-all-done.2 = f32[32,1,512]{2,1,0:T(1,128)S(1)} async-done(((f32[32,1,512]{2,1,0:T(1,128)}), f32[32,1,512]{2,1,0:T(1,128)S(1)}, u32[]{:S(2)}, u32[]{:S(2)}) %all-to-all-start.2) | async-done | bytes 65568 | tf_op jit(solution)/shard_map/all_to_all | solution.py:25
  60.9 0.1 add_bitcast_fusion
  61.0 1.4 %copy.25 = f32[8,1,16384]{2,1,0:T(1,128)} copy(f32[8,1,16384]{2,0,1:T(8,128)S(1)} %add_bitcast_fusion) | data formatting | bytes 1048576 | tf_op jit(solution)/shard_map/all_to_all | solution.py:27
  62.4 7.0 %all-to-all-start.3 = ((f32[8,1,16384]{2,1,0:T(1,128)}), f32[8,1,16384]{2,1,0:T(1,128)S(1)}, u32[]{:S(2)}, u32[]{:S(2)}) async-start(f32[8,1,16384]{2,1,0:T(1,128)} %copy.25), calls=%async_computation.3 | async-start | bytes 1048576 | tf_op jit(solution)/shard_map/all_to_all | solution.py:27
  69.3 6.4 %fusion.3 = f32[8,8,128,128]{2,3,1,0:T(8,128)} fusion(bf16[8,128,8,128]{3,2,1,0:T(8,128)(2,1)} %bitcast.40, bf16[8,128,8,128]{1,3,2,0:T(8,128)(2,1)S(1)} %copy.20, pred[128,128]{1,0:T(8,128)(4,1)S(1)} %iota_compare_fusion, bf16[8,128,8,128]{3,2,1,0:T(8,128)(2,1)} %bitcast.41), kind=kOutput, calls=%fused_computation.9 | convolution fusion | flops 538968064 | bytes 10502144 | tf_op jit(solution)/shard_map/nhcs,nshd->nchd/dot_general | solution.py:51
  75.7 3.0 %all-to-all-done.3 = f32[8,1,16384]{2,1,0:T(1,128)S(1)} async-done(((f32[8,1,16384]{2,1,0:T(1,128)}), f32[8,1,16384]{2,1,0:T(1,128)S(1)}, u32[]{:S(2)}, u32[]{:S(2)}) %all-to-all-start.3) | async-done | bytes 524320 | tf_op jit(solution)/shard_map/all_to_all | solution.py:27
  78.7 0.0 copy-start.2
  78.7 5.5 %multiply_reduce_fusion = (f32[8,128,8]{1,2,0:T(8,128)S(1)}, f32[8,128,8,128]{1,3,2,0:T(8,128)S(1)}) fusion(bf16[8,128,8,128]{3,2,1,0:T(8,128)(2,1)} %bitcast.42, f32[7,8,128,128]{3,2,1,0:T(8,128)} %slice.19, f32[8,128,128]{2,1,0:T(8,128)S(1)} %bitcast.45, f32[8,8,128,128]{2,3,1,0:T(8,128)} %fusion.3), kind=kOutput, calls=%fused_computation.2 | convolution fusion | flops 273670144 | bytes 14712832 | tf_op jit(solution)/shard_map/nchd,nhde->nche/dot_general | solution.py:56
  84.3 0.0 copy-done.2
  84.3 0.8 multiply_convert_fusion
  85.1 2.8 %copy.28 = bf16[8,128,8,128]{3,2,1,0:T(8,128)(2,1)} copy(bf16[8,128,8,128]{1,3,2,0:T(8,128)(2,1)S(1)} %multiply_convert_fusion) | data formatting | bytes 4194304 | tf_op jit(solution)/shard_map/convert_element_type | solution.py:62
  87.9 9.3 %convolution_convert_fusion = bf16[1024,2048]{1,0:T(8,128)(2,1)} fusion(bf16[1024,2048]{1,0:T(8,128)(2,1)} %param.9, bf16[128,8,8,128]{3,2,1,0:T(8,128)(2,1)} %bitcast.50), kind=kOutput, calls=%fused_computation.5 | convolution fusion | flops 4297064448 | bytes 10485760 | tf_op jit(solution)/shard_map/dot_general | solution.py:63
  (4 shorter events, 0.0 us)
Async XLA Ops:
  9.0 2.8 %copy-start = (bf16[128,8,8,128]{3,2,1,0:T(8,128)(2,1)}, bf16[128,8,8,128]{3,2,1,0:T(8,128)(2,1)S(1)}, u32[]{:S(2)}) copy-start(bf16[128,8,8,128]{3,2,1,0:T(8,128)(2,1)S(1)} %copy.34) | copy-start | bytes 6291460
  48.2 12.7 %all-to-all-start.2 = ((f32[32,1,512]{2,1,0:T(1,128)}), f32[32,1,512]{2,1,0:T(1,128)S(1)}, u32[]{:S(2)}, u32[]{:S(2)}) async-start(f32[32,1,512]{2,1,0:T(1,128)} %copy.24), calls=%async_computation.2 | async-start | bytes 131072 | tf_op jit(solution)/shard_map/all_to_all | solution.py:25
  54.6 2.5 %copy-start.1 = (bf16[1024,1024]{1,0:T(8,128)(2,1)S(1)}, bf16[1024,1024]{1,0:T(8,128)(2,1)}, u32[]{:S(2)}) copy-start(bf16[1024,1024]{1,0:T(8,128)(2,1)} %param.5) | copy-start | bytes 6291460
  62.4 16.4 %all-to-all-start.3 = ((f32[8,1,16384]{2,1,0:T(1,128)}), f32[8,1,16384]{2,1,0:T(1,128)S(1)}, u32[]{:S(2)}, u32[]{:S(2)}) async-start(f32[8,1,16384]{2,1,0:T(1,128)} %copy.25), calls=%async_computation.3 | async-start | bytes 1048576 | tf_op jit(solution)/shard_map/all_to_all | solution.py:27
  78.7 5.6 %copy-start.2 = (f32[1024]{0:T(1024)S(1)}, f32[1024]{0:T(1024)}, u32[]{:S(2)}) copy-start(f32[1024]{0:T(1024)} %param.8) | copy-start | bytes 12292

commit v2 on v1

v2 whole, which is shorter than its diff:
```python
import jax
import jax.numpy as jnp
from jax import lax
from jax.experimental import pallas as pl
from jax.experimental.pallas import tpu as pltpu
from jax.sharding import PartitionSpec as P

H = 8
DH = 128
C = 128


def exclusive_cumsum(rows):
    running = jnp.cumsum(rows, axis=0)
    return jnp.concatenate([jnp.zeros_like(rows[:1]), running[:-1]], axis=0), running[-1]


def carried_state(local_total):
    n_inner = lax.axis_size("inner")
    n_outer = lax.axis_size("outer")
    size = local_total.size
    chunks = local_total.reshape(n_inner, size // n_inner)
    gathered = lax.all_to_all(chunks, "inner", 0, 0, tiled=True)
    inner_before, group_total = exclusive_cumsum(gathered)
    pieces = lax.all_to_all(group_total.reshape(n_outer, -1), "outer", 0, 0, tiled=True)
    outer_before, _ = exclusive_cumsum(pieces)
    outer_chunk = lax.all_to_all(outer_before, "outer", 0, 0, tiled=True).reshape(-1)
    summed = inner_before + outer_chunk[None, :]
    back = lax.all_to_all(summed, "inner", 0, 0, tiled=True)
    return back.reshape(local_total.shape)


TILE = 256


def state_kernel(k_ref, v_ref, out_ref):
    for h in range(H):
        cols = slice(h * DH, (h + 1) * DH)
        out_ref[h] = lax.dot_general(
            k_ref[:, cols], v_ref[:, cols], (((0,), (0,)), ((), ())),
            preferred_element_type=jnp.float32,
        )


def state_totals(keys, values):
    rows = keys.shape[0]
    return pl.pallas_call(
        state_kernel,
        out_shape=jax.ShapeDtypeStruct((H, DH, DH), jnp.float32),
        grid=(1,),
        in_specs=[
            pl.BlockSpec((rows, H * DH), lambda i: (0, 0)),
            pl.BlockSpec((rows, H * DH), lambda i: (0, 0)),
        ],
        out_specs=pl.BlockSpec((H, DH, DH), lambda i: (0, 0, 0)),
    )(keys, values)


def layer_kernel(q_ref, k_ref, v_ref, c_ref, g_ref, w_ref, o_ref, run_ref, n_ref):
    @pl.when(pl.program_id(0) == 0)
    def _():
        run_ref[...] = c_ref[...]

    causal = lax.broadcasted_iota(jnp.int32, (C, C), 0) >= lax.broadcasted_iota(jnp.int32, (C, C), 1)
    for b in range(TILE // C):
        rows = slice(b * C, (b + 1) * C)
        for h in range(H):
            cols = slice(h * DH, (h + 1) * DH)
            qb = q_ref[rows, cols]
            kb = k_ref[rows, cols]
            vb = v_ref[rows, cols]
            scores = lax.dot_general(
                qb, kb, (((1,), (1,)), ((), ())), preferred_element_type=jnp.float32
            )
            weights = jnp.where(causal, scores, 0.0).astype(jnp.bfloat16)
            inside = jnp.dot(weights, vb, preferred_element_type=jnp.float32)
            prev = run_ref[h]
            carried_term = jnp.dot(qb, prev.astype(jnp.bfloat16), preferred_element_type=jnp.float32)
            attended = inside + carried_term
            mean_square = jnp.mean(attended * attended, axis=-1, keepdims=True)
            normed = attended * lax.rsqrt(mean_square + 1e-06) * g_ref[:, cols]
            n_ref[rows, cols] = normed.astype(jnp.bfloat16)
            run_ref[h] = prev + lax.dot_general(
                kb, vb, (((0,), (0,)), ((), ())), preferred_element_type=jnp.float32
            )
    o_ref[...] = jnp.dot(n_ref[...], w_ref[...], preferred_element_type=jnp.float32).astype(
        jnp.bfloat16
    )


def layer(queries, keys, values, carried, norm_gain, out_weight):
    rows, width = queries.shape
    out_width = out_weight.shape[1]
    tok = lambda t: (t, 0)
    fixed2 = lambda t: (0, 0)
    return pl.pallas_call(
        layer_kernel,
        out_shape=jax.ShapeDtypeStruct((rows, out_width), jnp.bfloat16),
        grid=(rows // TILE,),
        in_specs=[
            pl.BlockSpec((TILE, width), tok),
            pl.BlockSpec((TILE, width), tok),
            pl.BlockSpec((TILE, width), tok),
            pl.BlockSpec((H, DH, DH), lambda t: (0, 0, 0)),
            pl.BlockSpec((1, width), fixed2),
            pl.BlockSpec((width, out_width), fixed2),
        ],
        out_specs=pl.BlockSpec((TILE, out_width), tok),
        scratch_shapes=[
            pltpu.VMEM((H, DH, DH), jnp.float32),
            pltpu.VMEM((TILE, width), jnp.bfloat16),
        ],
        compiler_params=pltpu.CompilerParams(dimension_semantics=("arbitrary",)),
    )(queries, keys, values, carried, norm_gain.reshape(1, width), out_weight)


def on_device(queries, keys, values, norm_gain, out_weight):
    local_total = state_totals(keys, values)
    carried = carried_state(local_total)
    return layer(queries, keys, values, carried, norm_gain, out_weight)


def solution(mesh):
    return jax.shard_map(
        on_device,
        mesh=mesh,
        in_specs=(
            P(("outer", "inner"), None),
            P(("outer", "inner"), None),
            P(("outer", "inner"), None),
            P(),
            P(),
        ),
        out_specs=P(("outer", "inner"), None),
        check_vma=False,
    )
```

time: 97.8 us -> 88 us (0.90)
  blocking collectives: 34.7 us -> 62.9 us
  matrix products: 24 us -> 0 us
  Pallas kernels: 0 us -> 23.2 us
  local copies, waits for them, and re-layouts: 18.7 us -> 0.99 us
  starting transfers between devices: 10.8 us -> 0 us
  waiting for transfers between devices: 4.86 us -> 0 us
  other arithmetic: 3.98 us -> 0.64 us
    all_to_all x0 -> x2, blocking collectives: none -> 28 us  [the longest x1 16 us: carried_state(): back = lax.all_to_all(summed, 'inner', 0, 0, tiled=True)]
    dot_general x4 -> x0, matrix products: 24 us -> none  [the longest x1 9.33 us: on_device(): jnp.dot(normed, out_weight, preferred_element_type=jnp.float32)]
    pallas_call x0 -> x2, Pallas kernels: none -> 23.2 us  [the longest x1 19.1 us: layer(): pl.pallas_call(layer_kernel, out_shape=jax.ShapeDtypeStruct((rows, out_wi...]
    all_to_all x2 -> x0, starting transfers between devices: 10.8 us -> none  [the longest x1 6.97 us: carried_state(): back = lax.all_to_all(summed, 'inner', 0, 0, tiled=True)]
    unnamed x11 -> x2, local copies, waits for them, and re-layouts: 8.49 us -> 0.31 us
    all_to_all x2 -> x0, waiting for transfers between devices: 4.86 us -> none  [the longest x1 2.99 us: carried_state(): back = lax.all_to_all(summed, 'inner', 0, 0, tiled=True)]
    reshape x1 -> x0, local copies, waits for them, and re-layouts: 3.27 us -> none  [on_device(): key_blocks = keys.reshape(blocks, C, H, DH)]
    convert_element_type x1 -> x0, local copies, waits for them, and re-layouts: 2.82 us -> none  [on_device(): normed = normed.astype(jnp.bfloat16).reshape(tok_rows, H * DH)]
  transfers between devices with their start and end apart: 2 -> 0, of which waited for: 2 -> 0; matrix products, arithmetic and copies ran while one was open for 13% -> 0% of each run, Pallas kernels for 0% -> 0%
where the time goes in v2:
time: 88 us; the launch traced here: 87.8 us
  blocking collectives  62.9 us (71%)
  Pallas kernels  23.2 us (26%)
  local copies, waits for them, and re-layouts  0.99 us (1%)
    pallas_call x1, Pallas kernels, layer(): pl.pallas_call(layer_kernel, out_shape=jax.ShapeDtypeStruct((rows, out_wi...  19.1 us
    all_to_all x1, blocking collectives, carried_state(): lax.all_to_all(group_total.reshape(n_outer, -1), 'outer', 0, 0, tiled=True)  19 us
    all_to_all x1, blocking collectives, carried_state(): back = lax.all_to_all(summed, 'inner', 0, 0, tiled=True)  16 us
    all_to_all x1, blocking collectives, carried_state(): gathered = lax.all_to_all(chunks, 'inner', 0, 0, tiled=True)  15.9 us
    all_to_all x1, blocking collectives, carried_state(): lax.all_to_all(outer_before, 'outer', 0, 0, tiled=True).reshape(-1)  11.9 us
    pallas_call x1, Pallas kernels, state_totals(): pl.pallas_call(state_kernel, out_shape=jax.ShapeDtypeStruct((H, DH, DH),...  4.06 us

profile of v2, /device:TPU:1, one launch (start us, length us, event | category | flops | bytes accessed | tf_op | source)
XLA Modules:
  0.0 87.8 jit_solution(18107907805344158015)
XLA Ops:
  0.0 4.1 %shard_map.55 = f32[8,128,128]{2,1,0:T(8,128)} custom-call(bf16[1024,1024]{1,0:T(8,128)(2,1)} %k_ref.3, bf16[1024,1024]{1,0:T(8,128)(2,1)} %v_ref.3), custom_call_target="tpu_custom_call" | custom-call | tf_op jit(solution)/shard_map/pallas_call | solution.py:47
  4.1 15.9 %all_to_all.42 = f32[8,1,16384]{2,1,0:T(1,128)S(1)} all-to-all(f32[8,1,16384]{2,1,0:T(1,128)} %bitcast.19), channel_id=1, replica_groups=mesh['outer'=32,'inner'=8] {'inner'}, dimensions={0} | all-to-all | bytes 1048576 | tf_op jit(solution)/shard_map/all_to_all | solution.py:23
  20.0 0.3 copy.14
  20.3 0.5 reduce_window_sum.22
  20.7 0.1 slice.13
  20.8 19.0 %all_to_all.43 = f32[32,1,512]{2,1,0:T(1,128)S(1)} all-to-all(f32[32,1,512]{2,1,0:T(1,128)S(1)} %bitcast.24), channel_id=1, replica_groups=mesh['outer'=32,'inner'=8] {'outer'}, dimensions={0} | all-to-all | bytes 131072 | tf_op jit(solution)/shard_map/all_to_all | solution.py:25
  39.9 0.1 reduce_window_sum.23
  39.9 0.1 copy.8
  40.0 11.9 %all_to_all.44 = f32[32,1,512]{2,1,0:T(1,128)S(1)} all-to-all(f32[32,1,512]{2,1,0:T(1,128)S(1)} %copy.8), channel_id=1, replica_groups=mesh['outer'=32,'inner'=8] {'outer'}, dimensions={0} | all-to-all | bytes 131072 | tf_op jit(solution)/shard_map/all_to_all | solution.py:27
  52.0 0.1 add_bitcast_fusion
  52.1 0.5 copy.9
  52.6 16.0 %all_to_all.45 = f32[8,1,16384]{2,1,0:T(1,128)} all-to-all(f32[8,1,16384]{2,1,0:T(1,128)S(1)} %copy.9), channel_id=1, replica_groups=mesh['outer'=32,'inner'=8] {'inner'}, dimensions={0} | all-to-all | bytes 1048576 | tf_op jit(solution)/shard_map/all_to_all | solution.py:29
  68.6 19.1 %shard_map.56 = bf16[1024,2048]{1,0:T(8,128)(2,1)} custom-call(bf16[1024,1024]{1,0:T(8,128)(2,1)} %q_ref.1, bf16[1024,1024]{1,0:T(8,128)(2,1)} %k_ref.3, bf16[1024,1024]{1,0:T(8,128)(2,1)} %v_ref.3, f32[8,128,128]{2,1,0:T(8,128)} %bitcast.18, f32[1,1024]{1,0:T(1,128)} %bitcast.25, bf16[1024,2048]{1,0:T(8,128)(2,1)} %w_ref.1), custom_call_target="tpu_custom_call" | custom-call | tf_op jit(solution)/shard_map/pallas_call | solution.py:96
  (2 shorter events, 0.0 us)

commit v3 on v2

--- a/solution.py
+++ b/solution.py
@@ -34,61 +34,86 @@
 
 
 def state_kernel(k_ref, v_ref, out_ref):
+    @pl.when(pl.program_id(0) == 0)
+    def _():
+        out_ref[...] = jnp.zeros_like(out_ref)
+
     for h in range(H):
         cols = slice(h * DH, (h + 1) * DH)
-        out_ref[h] = lax.dot_general(
+        out_ref[h] += lax.dot_general(
             k_ref[:, cols], v_ref[:, cols], (((0,), (0,)), ((), ())),
             preferred_element_type=jnp.float32,
         )
 
 
 def state_totals(keys, values):
-    rows = keys.shape[0]
+    rows, width = keys.shape
     return pl.pallas_call(
         state_kernel,
         out_shape=jax.ShapeDtypeStruct((H, DH, DH), jnp.float32),
-        grid=(1,),
+        grid=(rows // TILE,),
         in_specs=[
-            pl.BlockSpec((rows, H * DH), lambda i: (0, 0)),
-            pl.BlockSpec((rows, H * DH), lambda i: (0, 0)),
+            pl.BlockSpec((TILE, width), lambda t: (t, 0)),
+            pl.BlockSpec((TILE, width), lambda t: (t, 0)),
         ],
-        out_specs=pl.BlockSpec((H, DH, DH), lambda i: (0, 0, 0)),
+        out_specs=pl.BlockSpec((H, DH, DH), lambda t: (0, 0, 0)),
+        compiler_params=pltpu.CompilerParams(dimension_semantics=("arbitrary",)),
     )(keys, values)
 
 
-def layer_kernel(q_ref, k_ref, v_ref, c_ref, g_ref, w_ref, o_ref, run_ref, n_ref):
-    @pl.when(pl.program_id(0) == 0)
-    def _():
-        run_ref[...] = c_ref[...]
-
+def intra_kernel(q_ref, k_ref, v_ref, out_ref):
     causal = lax.broadcasted_iota(jnp.int32, (C, C), 0) >= lax.broadcasted_iota(jnp.int32, (C, C), 1)
     for b in range(TILE // C):
         rows = slice(b * C, (b + 1) * C)
         for h in range(H):
             cols = slice(h * DH, (h + 1) * DH)
-            qb = q_ref[rows, cols]
-            kb = k_ref[rows, cols]
             vb = v_ref[rows, cols]
             scores = lax.dot_general(
-                qb, kb, (((1,), (1,)), ((), ())), preferred_element_type=jnp.float32
+                q_ref[rows, cols], k_ref[rows, cols], (((1,), (1,)), ((), ())),
+                preferred_element_type=jnp.float32,
             )
             weights = jnp.where(causal, scores, 0.0).astype(jnp.bfloat16)
-            inside = jnp.dot(weights, vb, preferred_element_type=jnp.float32)
+            out_ref[rows, cols] = jnp.dot(weights, vb, preferred_element_type=jnp.float32)
+
+
+def intra_block(queries, keys, values):
+    rows, width = queries.shape
+    tok = lambda t: (t, 0)
+    return pl.pallas_call(
+        intra_kernel,
+        out_shape=jax.ShapeDtypeStruct((rows, width), jnp.float32),
+        grid=(rows // TILE,),
+        in_specs=[pl.BlockSpec((TILE, width), tok)] * 3,
+        out_specs=pl.BlockSpec((TILE, width), tok),
+    )(queries, keys, values)
+
+
+def layer_kernel(q_ref, k_ref, v_ref, i_ref, c_ref, g_ref, w_ref, o_ref, run_ref, n_ref):
+    @pl.when(pl.program_id(0) == 0)
+    def _():
+        run_ref[...] = c_ref[...]
+
+    for b in range(TILE // C):
+        rows = slice(b * C, (b + 1) * C)
+        for h in range(H):
+            cols = slice(h * DH, (h + 1) * DH)
+            qb = q_ref[rows, cols]
             prev = run_ref[h]
             carried_term = jnp.dot(qb, prev.astype(jnp.bfloat16), preferred_element_type=jnp.float32)
-            attended = inside + carried_term
+            attended = i_ref[rows, cols] + carried_term
             mean_square = jnp.mean(attended * attended, axis=-1, keepdims=True)
             normed = attended * lax.rsqrt(mean_square + 1e-06) * g_ref[:, cols]
             n_ref[rows, cols] = normed.astype(jnp.bfloat16)
             run_ref[h] = prev + lax.dot_general(
-                kb, vb, (((0,), (0,)), ((), ())), preferred_element_type=jnp.float32
+                k_ref[rows, cols], v_ref[rows, cols], (((0,), (0,)), ((), ())),
+                preferred_element_type=jnp.float32,
             )
     o_ref[...] = jnp.dot(n_ref[...], w_ref[...], preferred_element_type=jnp.float32).astype(
         jnp.bfloat16
     )
 
 
-def layer(queries, keys, values, carried, norm_gain, out_weight):
+def layer(queries, keys, values, inside, carried, norm_gain, out_weight):
     rows, width = queries.shape
     out_width = out_weight.shape[1]
     tok = lambda t: (t, 0)
@@ -98,6 +123,7 @@
         out_shape=jax.ShapeDtypeStruct((rows, out_width), jnp.bfloat16),
         grid=(rows // TILE,),
         in_specs=[
+            pl.BlockSpec((TILE, width), tok),
             pl.BlockSpec((TILE, width), tok),
             pl.BlockSpec((TILE, width), tok),
             pl.BlockSpec((TILE, width), tok),
@@ -111,13 +137,14 @@
             pltpu.VMEM((TILE, width), jnp.bfloat16),
         ],
         compiler_params=pltpu.CompilerParams(dimension_semantics=("arbitrary",)),
-    )(queries, keys, values, carried, norm_gain.reshape(1, width), out_weight)
+    )(queries, keys, values, inside, carried, norm_gain.reshape(1, width), out_weight)
 
 
 def on_device(queries, keys, values, norm_gain, out_weight):
     local_total = state_totals(keys, values)
+    inside = intra_block(queries, keys, values)
     carried = carried_state(local_total)
-    return layer(queries, keys, values, carried, norm_gain, out_weight)
+    return layer(queries, keys, values, inside, carried, norm_gain, out_weight)
 
 
 def solution(mesh):

time: 88 us -> 86.4 us (0.982)
  blocking collectives: 62.9 us -> 46.9 us
  starting transfers between devices: 0 us -> 7.02 us
  Pallas kernels: 23.2 us -> 28.8 us
  local copies, waits for them, and re-layouts: 0.99 us -> 2.58 us
    all_to_all x1 -> x0, blocking collectives: 16 us -> none  [carried_state(): back = lax.all_to_all(summed, 'inner', 0, 0, tiled=True)]
    pallas_call x0 -> x1, Pallas kernels: none -> 12.7 us  [intra_block(): pl.pallas_call(intra_kernel, out_shape=jax.ShapeDtypeStruct((rows, width)...]
    pallas_call x1, Pallas kernels: 19.1 us -> 11.7 us  [layer(): pl.pallas_call(layer_kernel, out_shape=jax.ShapeDtypeStruct((rows, out_wi...]
    all_to_all x0 -> x1, starting transfers between devices: none -> 7.02 us  [carried_state(): back = lax.all_to_all(summed, 'inner', 0, 0, tiled=True)]
  transfers between devices with their start and end apart: 0 -> 1, of which waited for: 0 -> 0; matrix products, arithmetic and copies ran while one was open for 0% -> 0% of each run, Pallas kernels for 0% -> 15%
where the time goes in v3:
time: 86.4 us; the launch traced here: 86 us
  blocking collectives  46.9 us (54%)
  Pallas kernels  28.8 us (33%)
  starting transfers between devices  7.02 us (8%)
  local copies, waits for them, and re-layouts  2.58 us (3%)
    all_to_all x1, blocking collectives, carried_state(): lax.all_to_all(group_total.reshape(n_outer, -1), 'outer', 0, 0, tiled=True)  19 us
    all_to_all x1, blocking collectives, carried_state(): gathered = lax.all_to_all(chunks, 'inner', 0, 0, tiled=True)  15.9 us
    pallas_call x1, Pallas kernels, intra_block(): pl.pallas_call(intra_kernel, out_shape=jax.ShapeDtypeStruct((rows, width)...  12.7 us
    all_to_all x1, blocking collectives, carried_state(): lax.all_to_all(outer_before, 'outer', 0, 0, tiled=True).reshape(-1)  11.9 us
    pallas_call x1, Pallas kernels, layer(): pl.pallas_call(layer_kernel, out_shape=jax.ShapeDtypeStruct((rows, out_wi...  11.7 us
    all_to_all x1, starting transfers between devices, carried_state(): back = lax.all_to_all(summed, 'inner', 0, 0, tiled=True)  7.02 us
    pallas_call x1, Pallas kernels, state_totals(): pl.pallas_call(state_kernel, out_shape=jax.ShapeDtypeStruct((H, DH, DH),...  4.4 us
  transfers between devices with their start and end apart: 1, of which 0 were waited for; matrix products, arithmetic and copies ran while one was open for 0% of the time, Pallas kernels for 15%

profile of v3, /device:TPU:1, one launch (start us, length us, event | category | flops | bytes accessed | tf_op | source)
XLA Modules:
  0.0 86.0 jit_solution(5414709954929819725)
XLA Ops:
  0.0 4.4 %shard_map.56 = f32[8,128,128]{2,1,0:T(8,128)} custom-call(bf16[1024,1024]{1,0:T(8,128)(2,1)} %k_ref.5, bf16[1024,1024]{1,0:T(8,128)(2,1)} %v_ref.5), custom_call_target="tpu_custom_call" | custom-call | tf_op jit(solution)/shard_map/pallas_call | solution.py:51
  4.4 15.9 %all_to_all.42 = f32[8,1,16384]{2,1,0:T(1,128)S(1)} all-to-all(f32[8,1,16384]{2,1,0:T(1,128)} %bitcast.18), channel_id=1, replica_groups=mesh['outer'=32,'inner'=8] {'inner'}, dimensions={0} | all-to-all | bytes 1048576 | tf_op jit(solution)/shard_map/all_to_all | solution.py:23
  20.3 0.3 copy.14
  20.6 0.5 reduce_window_sum.22
  21.1 0.1 slice.13
  21.2 19.0 %all_to_all.43 = f32[32,1,512]{2,1,0:T(1,128)S(1)} all-to-all(f32[32,1,512]{2,1,0:T(1,128)S(1)} %bitcast.24), channel_id=1, replica_groups=mesh['outer'=32,'inner'=8] {'outer'}, dimensions={0} | all-to-all | bytes 131072 | tf_op jit(solution)/shard_map/all_to_all | solution.py:25
  40.2 0.1 reduce_window_sum.23
  40.3 0.1 copy.8
  40.4 11.9 %all_to_all.44 = f32[32,1,512]{2,1,0:T(1,128)S(1)} all-to-all(f32[32,1,512]{2,1,0:T(1,128)S(1)} %copy.8), channel_id=1, replica_groups=mesh['outer'=32,'inner'=8] {'outer'}, dimensions={0} | all-to-all | bytes 131072 | tf_op jit(solution)/shard_map/all_to_all | solution.py:27
  52.3 0.1 add_bitcast_fusion
  52.4 1.3 %copy.9 = f32[8,1,16384]{2,1,0:T(1,128)} copy(f32[8,1,16384]{2,0,1:T(8,128)S(1)} %add_bitcast_fusion) | data formatting | bytes 1048576 | tf_op jit(solution)/shard_map/all_to_all | solution.py:29
  53.7 7.0 %all-to-all-start.3 = ((f32[8,1,16384]{2,1,0:T(1,128)}), f32[8,1,16384]{2,1,0:T(1,128)S(1)}, u32[]{:S(2)}, u32[]{:S(2)}) async-start(f32[8,1,16384]{2,1,0:T(1,128)} %copy.9), calls=%async_computation.3 | async-start | bytes 1048576 | tf_op jit(solution)/shard_map/all_to_all | solution.py:29
  60.8 12.7 %shard_map.55.i_ref = f32[1024,1024]{1,0:T(8,128)} custom-call(bf16[1024,1024]{1,0:T(8,128)(2,1)} %q_ref.3, bf16[1024,1024]{1,0:T(8,128)(2,1)} %k_ref.5, bf16[1024,1024]{1,0:T(8,128)(2,1)} %v_ref.5), custom_call_target="tpu_custom_call" | custom-call | tf_op jit(solution)/shard_map/pallas_call | solution.py:82
  73.4 0.0 all-to-all-done.3
  73.4 0.0 copy-start
  73.5 0.8 copy-done
  74.2 11.7 %shard_map.57 = bf16[1024,2048]{1,0:T(8,128)(2,1)} custom-call(bf16[1024,1024]{1,0:T(8,128)(2,1)} %q_ref.3, bf16[1024,1024]{1,0:T(8,128)(2,1)} %k_ref.5, bf16[1024,1024]{1,0:T(8,128)(2,1)} %v_ref.5, f32[1024,1024]{1,0:T(8,128)} %shard_map.55.i_ref, f32[8,128,128]{2,1,0:T(8,128)} %bitcast.20, f32[1,1024]{1,0:T(1,128)} %bitcast.25, bf16[1024,2048]{1,0:T(8,128)(2,1)} %w_ref.1), custom_call_target="tpu_custom_call" | custom-call | tf_op jit(solution)/shard_map/pallas_call | solution.py:121
  (2 shorter events, 0.0 us)
Async XLA Ops:
  53.7 19.7 %all-to-all-start.3 = ((f32[8,1,16384]{2,1,0:T(1,128)}), f32[8,1,16384]{2,1,0:T(1,128)S(1)}, u32[]{:S(2)}, u32[]{:S(2)}) async-start(f32[8,1,16384]{2,1,0:T(1,128)} %copy.9), calls=%async_computation.3 | async-start | bytes 1048576 | tf_op jit(solution)/shard_map/all_to_all | solution.py:29
  73.4 0.8 copy-start

commit v4 on v3

--- a/solution.py
+++ b/solution.py
@@ -31,6 +31,9 @@
 
 
 TILE = 256
+STATE_TILE = 512
+INTRA_TILE = 512
+PAIR = 2 * DH
 
 
 def state_kernel(k_ref, v_ref, out_ref):
@@ -51,10 +54,10 @@
     return pl.pallas_call(
         state_kernel,
         out_shape=jax.ShapeDtypeStruct((H, DH, DH), jnp.float32),
-        grid=(rows // TILE,),
+        grid=(rows // STATE_TILE,),
         in_specs=[
-            pl.BlockSpec((TILE, width), lambda t: (t, 0)),
-            pl.BlockSpec((TILE, width), lambda t: (t, 0)),
+            pl.BlockSpec((STATE_TILE, width), lambda t: (t, 0)),
+            pl.BlockSpec((STATE_TILE, width), lambda t: (t, 0)),
         ],
         out_specs=pl.BlockSpec((H, DH, DH), lambda t: (0, 0, 0)),
         compiler_params=pltpu.CompilerParams(dimension_semantics=("arbitrary",)),
@@ -62,18 +65,20 @@
 
 
 def intra_kernel(q_ref, k_ref, v_ref, out_ref):
-    causal = lax.broadcasted_iota(jnp.int32, (C, C), 0) >= lax.broadcasted_iota(jnp.int32, (C, C), 1)
-    for b in range(TILE // C):
-        rows = slice(b * C, (b + 1) * C)
+    span = 2 * C
+    row = lax.broadcasted_iota(jnp.int32, (span, span), 0)
+    col = lax.broadcasted_iota(jnp.int32, (span, span), 1)
+    causal = (row >= col) & (row // C == col // C)
+    for b in range(INTRA_TILE // span):
+        rows = slice(b * span, (b + 1) * span)
         for h in range(H):
             cols = slice(h * DH, (h + 1) * DH)
-            vb = v_ref[rows, cols]
             scores = lax.dot_general(
                 q_ref[rows, cols], k_ref[rows, cols], (((1,), (1,)), ((), ())),
                 preferred_element_type=jnp.float32,
             )
             weights = jnp.where(causal, scores, 0.0).astype(jnp.bfloat16)
-            out_ref[rows, cols] = jnp.dot(weights, vb, preferred_element_type=jnp.float32)
+            out_ref[rows, cols] = jnp.dot(weights, v_ref[rows, cols], preferred_element_type=jnp.float32)
 
 
 def intra_block(queries, keys, values):
@@ -82,32 +87,44 @@
     return pl.pallas_call(
         intra_kernel,
         out_shape=jax.ShapeDtypeStruct((rows, width), jnp.float32),
-        grid=(rows // TILE,),
-        in_specs=[pl.BlockSpec((TILE, width), tok)] * 3,
-        out_specs=pl.BlockSpec((TILE, width), tok),
+        grid=(rows // INTRA_TILE,),
+        in_specs=[pl.BlockSpec((INTRA_TILE, width), tok)] * 3,
+        out_specs=pl.BlockSpec((INTRA_TILE, width), tok),
     )(queries, keys, values)
 
 
 def layer_kernel(q_ref, k_ref, v_ref, i_ref, c_ref, g_ref, w_ref, o_ref, run_ref, n_ref):
+    row = lax.broadcasted_iota(jnp.int32, (PAIR, PAIR), 0)
+    col = lax.broadcasted_iota(jnp.int32, (PAIR, PAIR), 1)
+    same_head = row // DH == col // DH
+
     @pl.when(pl.program_id(0) == 0)
     def _():
-        run_ref[...] = c_ref[...]
+        run_ref[...] = jnp.zeros_like(run_ref)
+        for h in range(H):
+            at = slice((h % 2) * DH, (h % 2 + 1) * DH)
+            run_ref[h // 2, at, at] = c_ref[h]
 
     for b in range(TILE // C):
         rows = slice(b * C, (b + 1) * C)
-        for h in range(H):
-            cols = slice(h * DH, (h + 1) * DH)
-            qb = q_ref[rows, cols]
-            prev = run_ref[h]
-            carried_term = jnp.dot(qb, prev.astype(jnp.bfloat16), preferred_element_type=jnp.float32)
+        for p in range(H // 2):
+            cols = slice(p * PAIR, (p + 1) * PAIR)
+            prev = run_ref[p]
+            carried_term = jnp.dot(
+                q_ref[rows, cols], prev.astype(jnp.bfloat16), preferred_element_type=jnp.float32
+            )
             attended = i_ref[rows, cols] + carried_term
-            mean_square = jnp.mean(attended * attended, axis=-1, keepdims=True)
-            normed = attended * lax.rsqrt(mean_square + 1e-06) * g_ref[:, cols]
-            n_ref[rows, cols] = normed.astype(jnp.bfloat16)
-            run_ref[h] = prev + lax.dot_general(
+            for half in range(2):
+                part = attended[:, half * DH:(half + 1) * DH]
+                mean_square = jnp.mean(part * part, axis=-1, keepdims=True)
+                hcols = slice(p * PAIR + half * DH, p * PAIR + (half + 1) * DH)
+                normed = part * lax.rsqrt(mean_square + 1e-06) * g_ref[:, hcols]
+                n_ref[rows, hcols] = normed.astype(jnp.bfloat16)
+            update = lax.dot_general(
                 k_ref[rows, cols], v_ref[rows, cols], (((0,), (0,)), ((), ())),
                 preferred_element_type=jnp.float32,
             )
+            run_ref[p] = prev + jnp.where(same_head, update, 0.0)
     o_ref[...] = jnp.dot(n_ref[...], w_ref[...], preferred_element_type=jnp.float32).astype(
         jnp.bfloat16
     )
@@ -133,7 +150,7 @@
         ],
         out_specs=pl.BlockSpec((TILE, out_width), tok),
         scratch_shapes=[
-            pltpu.VMEM((H, DH, DH), jnp.float32),
+            pltpu.VMEM((H // 2, PAIR, PAIR), jnp.float32),
             pltpu.VMEM((TILE, width), jnp.bfloat16),
         ],
         compiler_params=pltpu.CompilerParams(dimension_semantics=("arbitrary",)),

time: 86.4 us -> 82.4 us (0.954)
  Pallas kernels: 28.8 us -> 21.6 us
  waiting for transfers between devices: 0.01 us -> 3.25 us
    pallas_call x1, Pallas kernels: 12.7 us -> 6.13 us  [intra_block(): pl.pallas_call(intra_kernel, out_shape=jax.ShapeDtypeStruct((rows, width)...]
    all_to_all x1, waiting for transfers between devices: 0.01 us -> 3.25 us  [carried_state(): back = lax.all_to_all(summed, 'inner', 0, 0, tiled=True)]
    pallas_call x1, Pallas kernels: 4.4 us -> 3.49 us  [state_totals(): pl.pallas_call(state_kernel, out_shape=jax.ShapeDtypeStruct((H, DH, DH),...]
  transfers between devices with their start and end apart: 1 -> 1, of which waited for: 0 -> 1; matrix products, arithmetic and copies ran while one was open for 0% -> 0% of each run, Pallas kernels for 15% -> 7%
where the time goes in v4:
time: 82.4 us; the launch traced here: 82 us
  blocking collectives  46.9 us (57%)
  Pallas kernels  21.6 us (26%)
  starting transfers between devices  7.02 us (9%)
  waiting for transfers between devices  3.25 us (4%)
  local copies, waits for them, and re-layouts  2.58 us (3%)
    all_to_all x1, blocking collectives, carried_state(): lax.all_to_all(group_total.reshape(n_outer, -1), 'outer', 0, 0, tiled=True)  19 us
    all_to_all x1, blocking collectives, carried_state(): gathered = lax.all_to_all(chunks, 'inner', 0, 0, tiled=True)  15.9 us
    pallas_call x1, Pallas kernels, layer(): pl.pallas_call(layer_kernel, out_shape=jax.ShapeDtypeStruct((rows, out_wi...  12 us
    all_to_all x1, blocking collectives, carried_state(): lax.all_to_all(outer_before, 'outer', 0, 0, tiled=True).reshape(-1)  11.9 us
    all_to_all x1, starting transfers between devices, carried_state(): back = lax.all_to_all(summed, 'inner', 0, 0, tiled=True)  7.02 us
    pallas_call x1, Pallas kernels, intra_block(): pl.pallas_call(intra_kernel, out_shape=jax.ShapeDtypeStruct((rows, width)...  6.13 us
    pallas_call x1, Pallas kernels, state_totals(): pl.pallas_call(state_kernel, out_shape=jax.ShapeDtypeStruct((H, DH, DH),...  3.49 us
    all_to_all x1, waiting for transfers between devices, carried_state(): back = lax.all_to_all(summed, 'inner', 0, 0, tiled=True)  3.25 us
  transfers between devices with their start and end apart: 1, of which 1 were waited for; matrix products, arithmetic and copies ran while one was open for 0% of the time, Pallas kernels for 7%

profile of v4, /device:TPU:1, one launch (start us, length us, event | category | flops | bytes accessed | tf_op | source)
XLA Modules:
  0.0 82.0 jit_solution(8176877944475019223)
XLA Ops:
  0.0 3.5 %shard_map.56 = f32[8,128,128]{2,1,0:T(8,128)} custom-call(bf16[1024,1024]{1,0:T(8,128)(2,1)} %k_ref.5, bf16[1024,1024]{1,0:T(8,128)(2,1)} %v_ref.5), custom_call_target="tpu_custom_call" | custom-call | tf_op jit(solution)/shard_map/pallas_call | solution.py:54
  3.5 15.9 %all_to_all.42 = f32[8,1,16384]{2,1,0:T(1,128)S(1)} all-to-all(f32[8,1,16384]{2,1,0:T(1,128)} %bitcast.18), channel_id=1, replica_groups=mesh['outer'=32,'inner'=8] {'inner'}, dimensions={0} | all-to-all | bytes 1048576 | tf_op jit(solution)/shard_map/all_to_all | solution.py:23
  19.4 0.3 copy.14
  19.7 0.5 reduce_window_sum.22
  20.2 0.1 slice.13
  20.2 19.0 %all_to_all.43 = f32[32,1,512]{2,1,0:T(1,128)S(1)} all-to-all(f32[32,1,512]{2,1,0:T(1,128)S(1)} %bitcast.24), channel_id=1, replica_groups=mesh['outer'=32,'inner'=8] {'outer'}, dimensions={0} | all-to-all | bytes 131072 | tf_op jit(solution)/shard_map/all_to_all | solution.py:25
  39.3 0.1 reduce_window_sum.23
  39.4 0.1 copy.8
  39.5 11.9 %all_to_all.44 = f32[32,1,512]{2,1,0:T(1,128)S(1)} all-to-all(f32[32,1,512]{2,1,0:T(1,128)S(1)} %copy.8), channel_id=1, replica_groups=mesh['outer'=32,'inner'=8] {'outer'}, dimensions={0} | all-to-all | bytes 131072 | tf_op jit(solution)/shard_map/all_to_all | solution.py:27
  51.4 0.1 add_bitcast_fusion
  51.5 1.3 %copy.9 = f32[8,1,16384]{2,1,0:T(1,128)} copy(f32[8,1,16384]{2,0,1:T(8,128)S(1)} %add_bitcast_fusion) | data formatting | bytes 1048576 | tf_op jit(solution)/shard_map/all_to_all | solution.py:29
  52.8 7.0 %all-to-all-start.3 = ((f32[8,1,16384]{2,1,0:T(1,128)}), f32[8,1,16384]{2,1,0:T(1,128)S(1)}, u32[]{:S(2)}, u32[]{:S(2)}) async-start(f32[8,1,16384]{2,1,0:T(1,128)} %copy.9), calls=%async_computation.3 | async-start | bytes 1048576 | tf_op jit(solution)/shard_map/all_to_all | solution.py:29
  59.9 6.1 %shard_map.55.i_ref = f32[1024,1024]{1,0:T(8,128)} custom-call(bf16[1024,1024]{1,0:T(8,128)(2,1)} %q_ref.3, bf16[1024,1024]{1,0:T(8,128)(2,1)} %k_ref.5, bf16[1024,1024]{1,0:T(8,128)(2,1)} %v_ref.5), custom_call_target="tpu_custom_call" | custom-call | tf_op jit(solution)/shard_map/pallas_call | solution.py:87
  66.0 3.2 %all-to-all-done.3 = f32[8,1,16384]{2,1,0:T(1,128)S(1)} async-done(((f32[8,1,16384]{2,1,0:T(1,128)}), f32[8,1,16384]{2,1,0:T(1,128)S(1)}, u32[]{:S(2)}, u32[]{:S(2)}) %all-to-all-start.3) | async-done | bytes 524320 | tf_op jit(solution)/shard_map/all_to_all | solution.py:29
  69.2 0.0 copy-start
  69.2 0.8 copy-done
  70.0 12.0 %shard_map.57 = bf16[1024,2048]{1,0:T(8,128)(2,1)} custom-call(bf16[1024,1024]{1,0:T(8,128)(2,1)} %q_ref.3, bf16[1024,1024]{1,0:T(8,128)(2,1)} %k_ref.5, bf16[1024,1024]{1,0:T(8,128)(2,1)} %v_ref.5, f32[1024,1024]{1,0:T(8,128)} %shard_map.55.i_ref, f32[8,128,128]{2,1,0:T(8,128)} %bitcast.20, f32[1,1024]{1,0:T(1,128)} %bitcast.25, bf16[1024,2048]{1,0:T(8,128)(2,1)} %w_ref.1), custom_call_target="tpu_custom_call" | custom-call | tf_op jit(solution)/shard_map/pallas_call | solution.py:138
  (2 shorter events, 0.0 us)
Async XLA Ops:
  52.8 16.4 %all-to-all-start.3 = ((f32[8,1,16384]{2,1,0:T(1,128)}), f32[8,1,16384]{2,1,0:T(1,128)S(1)}, u32[]{:S(2)}, u32[]{:S(2)}) async-start(f32[8,1,16384]{2,1,0:T(1,128)} %copy.9), calls=%async_computation.3 | async-start | bytes 1048576 | tf_op jit(solution)/shard_map/all_to_all | solution.py:29
  69.2 0.8 copy-start

commit v5 on v4

--- a/solution.py
+++ b/solution.py
@@ -64,7 +64,7 @@
     )(keys, values)
 
 
-def intra_kernel(q_ref, k_ref, v_ref, out_ref):
+def intra_kernel(q_ref, k_ref, v_ref, out_ref, within_ref, run_ref):
     span = 2 * C
     row = lax.broadcasted_iota(jnp.int32, (span, span), 0)
     col = lax.broadcasted_iota(jnp.int32, (span, span), 1)
@@ -80,57 +80,59 @@
             weights = jnp.where(causal, scores, 0.0).astype(jnp.bfloat16)
             out_ref[rows, cols] = jnp.dot(weights, v_ref[rows, cols], preferred_element_type=jnp.float32)
 
+    @pl.when(pl.program_id(0) == 0)
+    def _():
+        run_ref[...] = jnp.zeros_like(run_ref)
+
+    for b in range(INTRA_TILE // C):
+        rows = slice(b * C, (b + 1) * C)
+        for h in range(H):
+            cols = slice(h * DH, (h + 1) * DH)
+            prev = run_ref[h]
+            within_ref[b, h] = prev
+            run_ref[h] = prev + lax.dot_general(
+                k_ref[rows, cols], v_ref[rows, cols], (((0,), (0,)), ((), ())),
+                preferred_element_type=jnp.float32,
+            )
+
 
 def intra_block(queries, keys, values):
     rows, width = queries.shape
     tok = lambda t: (t, 0)
     return pl.pallas_call(
         intra_kernel,
-        out_shape=jax.ShapeDtypeStruct((rows, width), jnp.float32),
+        out_shape=(
+            jax.ShapeDtypeStruct((rows, width), jnp.float32),
+            jax.ShapeDtypeStruct((rows // C, H, DH, DH), jnp.float32),
+        ),
         grid=(rows // INTRA_TILE,),
         in_specs=[pl.BlockSpec((INTRA_TILE, width), tok)] * 3,
-        out_specs=pl.BlockSpec((INTRA_TILE, width), tok),
+        out_specs=(
+            pl.BlockSpec((INTRA_TILE, width), tok),
+            pl.BlockSpec((INTRA_TILE // C, H, DH, DH), lambda t: (t, 0, 0, 0)),
+        ),
+        scratch_shapes=[pltpu.VMEM((H, DH, DH), jnp.float32)],
+        compiler_params=pltpu.CompilerParams(dimension_semantics=("arbitrary",)),
     )(queries, keys, values)
 
 
-def layer_kernel(q_ref, k_ref, v_ref, i_ref, c_ref, g_ref, w_ref, o_ref, run_ref, n_ref):
-    row = lax.broadcasted_iota(jnp.int32, (PAIR, PAIR), 0)
-    col = lax.broadcasted_iota(jnp.int32, (PAIR, PAIR), 1)
-    same_head = row // DH == col // DH
-
-    @pl.when(pl.program_id(0) == 0)
-    def _():
-        run_ref[...] = jnp.zeros_like(run_ref)
-        for h in range(H):
-            at = slice((h % 2) * DH, (h % 2 + 1) * DH)
-            run_ref[h // 2, at, at] = c_ref[h]
-
+def layer_kernel(q_ref, i_ref, w_in_ref, c_ref, g_ref, w_ref, o_ref, n_ref):
     for b in range(TILE // C):
         rows = slice(b * C, (b + 1) * C)
-        for p in range(H // 2):
-            cols = slice(p * PAIR, (p + 1) * PAIR)
-            prev = run_ref[p]
-            carried_term = jnp.dot(
-                q_ref[rows, cols], prev.astype(jnp.bfloat16), preferred_element_type=jnp.float32
-            )
+        for h in range(H):
+            cols = slice(h * DH, (h + 1) * DH)
+            prefix_low = (c_ref[h] + w_in_ref[b, h]).astype(jnp.bfloat16)
+            carried_term = jnp.dot(q_ref[rows, cols], prefix_low, preferred_element_type=jnp.float32)
             attended = i_ref[rows, cols] + carried_term
-            for half in range(2):
-                part = attended[:, half * DH:(half + 1) * DH]
-                mean_square = jnp.mean(part * part, axis=-1, keepdims=True)
-                hcols = slice(p * PAIR + half * DH, p * PAIR + (half + 1) * DH)
-                normed = part * lax.rsqrt(mean_square + 1e-06) * g_ref[:, hcols]
-                n_ref[rows, hcols] = normed.astype(jnp.bfloat16)
-            update = lax.dot_general(
-                k_ref[rows, cols], v_ref[rows, cols], (((0,), (0,)), ((), ())),
-                preferred_element_type=jnp.float32,
-            )
-            run_ref[p] = prev + jnp.where(same_head, update, 0.0)
+            mean_square = jnp.mean(attended * attended, axis=-1, keepdims=True)
+            normed = attended * lax.rsqrt(mean_square + 1e-06) * g_ref[:, cols]
+            n_ref[rows, cols] = normed.astype(jnp.bfloat16)
     o_ref[...] = jnp.dot(n_ref[...], w_ref[...], preferred_element_type=jnp.float32).astype(
         jnp.bfloat16
     )
 
 
-def layer(queries, keys, values, inside, carried, norm_gain, out_weight):
+def layer(queries, inside, within, carried, norm_gain, out_weight):
     rows, width = queries.shape
     out_width = out_weight.shape[1]
     tok = lambda t: (t, 0)
@@ -142,26 +144,21 @@
         in_specs=[
             pl.BlockSpec((TILE, width), tok),
             pl.BlockSpec((TILE, width), tok),
-            pl.BlockSpec((TILE, width), tok),
-            pl.BlockSpec((TILE, width), tok),
+            pl.BlockSpec((TILE // C, H, DH, DH), lambda t: (t, 0, 0, 0)),
             pl.BlockSpec((H, DH, DH), lambda t: (0, 0, 0)),
             pl.BlockSpec((1, width), fixed2),
             pl.BlockSpec((width, out_width), fixed2),
         ],
         out_specs=pl.BlockSpec((TILE, out_width), tok),
-        scratch_shapes=[
-            pltpu.VMEM((H // 2, PAIR, PAIR), jnp.float32),
-            pltpu.VMEM((TILE, width), jnp.bfloat16),
-        ],
-        compiler_params=pltpu.CompilerParams(dimension_semantics=("arbitrary",)),
-    )(queries, keys, values, inside, carried, norm_gain.reshape(1, width), out_weight)
+        scratch_shapes=[pltpu.VMEM((TILE, width), jnp.bfloat16)],
+    )(queries, inside, within, carried, norm_gain.reshape(1, width), out_weight)
 
 
 def on_device(queries, keys, values, norm_gain, out_weight):
     local_total = state_totals(keys, values)
-    inside = intra_block(queries, keys, values)
+    inside, within = intra_block(queries, keys, values)
     carried = carried_state(local_total)
-    return layer(queries, keys, values, inside, carried, norm_gain, out_weight)
+    return layer(queries, inside, within, carried, norm_gain, out_weight)
 
 
 def solution(mesh):

time: 82.4 us -> 82.1 us (level)
  waiting for transfers between devices: 3.25 us -> 1.94 us
  Pallas kernels: 21.6 us -> 22.5 us
    all_to_all x1, waiting for transfers between devices: 3.25 us -> 1.94 us  [carried_state(): back = lax.all_to_all(summed, 'inner', 0, 0, tiled=True)]
    pallas_call x1, Pallas kernels: 6.13 us -> 7.44 us  [intra_block(): pl.pallas_call(intra_kernel, out_shape=(jax.ShapeDtypeStruct((rows, width...]
  transfers between devices with their start and end apart: 1 -> 1, of which waited for: 1 -> 1; matrix products, arithmetic and copies ran while one was open for 0% -> 0% of each run, Pallas kernels for 7% -> 9%
where the time goes in v5:
time: 82.1 us; the launch traced here: 81.7 us
  blocking collectives  46.9 us (57%)
  Pallas kernels  22.5 us (27%)
  starting transfers between devices  7.02 us (9%)
  local copies, waits for them, and re-layouts  2.63 us (3%)
  waiting for transfers between devices  1.94 us (2%)
    all_to_all x1, blocking collectives, carried_state(): lax.all_to_all(group_total.reshape(n_outer, -1), 'outer', 0, 0, tiled=True)  19 us
    all_to_all x1, blocking collectives, carried_state(): gathered = lax.all_to_all(chunks, 'inner', 0, 0, tiled=True)  15.9 us
    all_to_all x1, blocking collectives, carried_state(): lax.all_to_all(outer_before, 'outer', 0, 0, tiled=True).reshape(-1)  11.9 us
    pallas_call x1, Pallas kernels, layer(): pl.pallas_call(layer_kernel, out_shape=jax.ShapeDtypeStruct((rows, out_wi...  11.6 us
    pallas_call x1, Pallas kernels, intra_block(): pl.pallas_call(intra_kernel, out_shape=(jax.ShapeDtypeStruct((rows, width...  7.44 us
    all_to_all x1, starting transfers between devices, carried_state(): back = lax.all_to_all(summed, 'inner', 0, 0, tiled=True)  7.02 us
    pallas_call x1, Pallas kernels, state_totals(): pl.pallas_call(state_kernel, out_shape=jax.ShapeDtypeStruct((H, DH, DH),...  3.49 us
    all_to_all x1, waiting for transfers between devices, carried_state(): back = lax.all_to_all(summed, 'inner', 0, 0, tiled=True)  1.94 us
  transfers between devices with their start and end apart: 1, of which 1 were waited for; matrix products, arithmetic and copies ran while one was open for 0% of the time, Pallas kernels for 9%

profile of v5, /device:TPU:1, one launch (start us, length us, event | category | flops | bytes accessed | tf_op | source)
XLA Modules:
  0.0 81.7 jit_solution(15200700746768971835)
XLA Ops:
  0.0 3.5 %shard_map.56 = f32[8,128,128]{2,1,0:T(8,128)} custom-call(bf16[1024,1024]{1,0:T(8,128)(2,1)} %k_ref.3, bf16[1024,1024]{1,0:T(8,128)(2,1)} %v_ref.3), custom_call_target="tpu_custom_call" | custom-call | tf_op jit(solution)/shard_map/pallas_call | solution.py:54
  3.5 15.9 %all_to_all.42 = f32[8,1,16384]{2,1,0:T(1,128)S(1)} all-to-all(f32[8,1,16384]{2,1,0:T(1,128)} %bitcast.18), channel_id=1, replica_groups=mesh['outer'=32,'inner'=8] {'inner'}, dimensions={0} | all-to-all | bytes 1048576 | tf_op jit(solution)/shard_map/all_to_all | solution.py:23
  19.4 0.3 copy.14
  19.7 0.5 reduce_window_sum.22
  20.2 0.1 slice.13
  20.2 19.0 %all_to_all.43 = f32[32,1,512]{2,1,0:T(1,128)S(1)} all-to-all(f32[32,1,512]{2,1,0:T(1,128)S(1)} %bitcast.24), channel_id=1, replica_groups=mesh['outer'=32,'inner'=8] {'outer'}, dimensions={0} | all-to-all | bytes 131072 | tf_op jit(solution)/shard_map/all_to_all | solution.py:25
  39.3 0.1 reduce_window_sum.23
  39.4 0.1 copy.8
  39.5 11.9 %all_to_all.44 = f32[32,1,512]{2,1,0:T(1,128)S(1)} all-to-all(f32[32,1,512]{2,1,0:T(1,128)S(1)} %copy.8), channel_id=1, replica_groups=mesh['outer'=32,'inner'=8] {'outer'}, dimensions={0} | all-to-all | bytes 131072 | tf_op jit(solution)/shard_map/all_to_all | solution.py:27
  51.4 0.1 add_bitcast_fusion
  51.5 1.3 %copy.9 = f32[8,1,16384]{2,1,0:T(1,128)} copy(f32[8,1,16384]{2,0,1:T(8,128)S(1)} %add_bitcast_fusion) | data formatting | bytes 1048576 | tf_op jit(solution)/shard_map/all_to_all | solution.py:29
  52.8 7.0 %all-to-all-start.3 = ((f32[8,1,16384]{2,1,0:T(1,128)}), f32[8,1,16384]{2,1,0:T(1,128)S(1)}, u32[]{:S(2)}, u32[]{:S(2)}) async-start(f32[8,1,16384]{2,1,0:T(1,128)} %copy.9), calls=%async_computation.3 | async-start | bytes 1048576 | tf_op jit(solution)/shard_map/all_to_all | solution.py:29
  59.9 7.4 %shard_map.55 = (f32[1024,1024]{1,0:T(8,128)}, f32[8,8,128,128]{3,2,1,0:T(8,128)}) custom-call(bf16[1024,1024]{1,0:T(8,128)(2,1)} %q_ref.3, bf16[1024,1024]{1,0:T(8,128)(2,1)} %k_ref.3, bf16[1024,1024]{1,0:T(8,128)(2,1)} %v_ref.3), custom_call_target="tpu_custom_call" | custom-call | tf_op jit(solution)/shard_map/pallas_call | solution.py:102
  67.3 1.9 %all-to-all-done.3 = f32[8,1,16384]{2,1,0:T(1,128)S(1)} async-done(((f32[8,1,16384]{2,1,0:T(1,128)}), f32[8,1,16384]{2,1,0:T(1,128)S(1)}, u32[]{:S(2)}, u32[]{:S(2)}) %all-to-all-start.3) | async-done | bytes 524320 | tf_op jit(solution)/shard_map/all_to_all | solution.py:29
  69.2 0.0 copy-start
  69.2 0.8 %copy-done = f32[8,1,16384]{2,1,0:T(1,128)} copy-done((f32[8,1,16384]{2,1,0:T(1,128)}, f32[8,1,16384]{2,1,0:T(1,128)S(1)}, u32[]{:S(2)}) %copy-start) | copy-done | bytes 524312
  70.1 11.6 %shard_map.57 = bf16[1024,2048]{1,0:T(8,128)(2,1)} custom-call(bf16[1024,1024]{1,0:T(8,128)(2,1)} %q_ref.3, f32[1024,1024]{1,0:T(8,128)} %get-tuple-element.7.i_ref, f32[8,8,128,128]{3,2,1,0:T(8,128)} %get-tuple-element.8.w_in_ref, f32[8,128,128]{2,1,0:T(8,128)} %bitcast.20, f32[1,1024]{1,0:T(1,128)} %bitcast.25, bf16[1024,2048]{1,0:T(8,128)(2,1)} %w_ref.1), custom_call_target="tpu_custom_call" | custom-call | tf_op jit(solution)/shard_map/pallas_call | solution.py:140
  (2 shorter events, 0.0 us)
Async XLA Ops:
  52.8 16.4 %all-to-all-start.3 = ((f32[8,1,16384]{2,1,0:T(1,128)}), f32[8,1,16384]{2,1,0:T(1,128)S(1)}, u32[]{:S(2)}, u32[]{:S(2)}) async-start(f32[8,1,16384]{2,1,0:T(1,128)} %copy.9), calls=%async_computation.3 | async-start | bytes 1048576 | tf_op jit(solution)/shard_map/all_to_all | solution.py:29
  69.2 0.8 %copy-start = (f32[8,1,16384]{2,1,0:T(1,128)}, f32[8,1,16384]{2,1,0:T(1,128)S(1)}, u32[]{:S(2)}) copy-start(f32[8,1,16384]{2,1,0:T(1,128)S(1)} %all-to-all-done.3) | copy-start | bytes 1572868

commit v6 on v5

--- a/solution.py
+++ b/solution.py
@@ -18,15 +18,15 @@
 def carried_state(local_total):
     n_inner = lax.axis_size("inner")
     n_outer = lax.axis_size("outer")
-    size = local_total.size
-    chunks = local_total.reshape(n_inner, size // n_inner)
-    gathered = lax.all_to_all(chunks, "inner", 0, 0, tiled=True)
+    lanes = local_total.shape[-1]
+    chunks = local_total.reshape(n_inner, -1, lanes)
+    gathered = lax.all_to_all(chunks, "inner", 0, 0, tiled=False)
     inner_before, group_total = exclusive_cumsum(gathered)
-    pieces = lax.all_to_all(group_total.reshape(n_outer, -1), "outer", 0, 0, tiled=True)
+    pieces = lax.all_to_all(group_total.reshape(n_outer, -1, lanes), "outer", 0, 0, tiled=False)
     outer_before, _ = exclusive_cumsum(pieces)
-    outer_chunk = lax.all_to_all(outer_before, "outer", 0, 0, tiled=True).reshape(-1)
-    summed = inner_before + outer_chunk[None, :]
-    back = lax.all_to_all(summed, "inner", 0, 0, tiled=True)
+    outer_chunk = lax.all_to_all(outer_before, "outer", 0, 0, tiled=False)
+    summed = inner_before + outer_chunk.reshape(1, -1, lanes)
+    back = lax.all_to_all(summed, "inner", 0, 0, tiled=False)
     return back.reshape(local_total.shape)
 
 

time: 82.1 us -> 82.4 us (level)
  blocking collectives: 46.9 us -> 34.9 us
  waiting for transfers between devices: 1.94 us -> 10.8 us
  starting transfers between devices: 7.02 us -> 10.8 us
  local copies, waits for them, and re-layouts: 2.63 us -> 1.53 us
    all_to_all x3 -> x2, blocking collectives: 46.9 us -> 34.9 us  [the longest x1 19 us: carried_state(): lax.all_to_all(group_total.reshape(n_outer, -1, lanes), 'outer', 0, 0, ti...]
    all_to_all x1 -> x2, waiting for transfers between devices: 1.94 us -> 10.8 us  [the longest x1 8.83 us: carried_state(): outer_chunk = lax.all_to_all(outer_before, 'outer', 0, 0, tiled=False)]
    all_to_all x1 -> x2, starting transfers between devices: 7.02 us -> 10.8 us  [the longest x1 6.97 us: carried_state(): back = lax.all_to_all(summed, 'inner', 0, 0, tiled=False)]
    all_to_all x3 -> x0, local copies, waits for them, and re-layouts: 1.41 us -> none  [the longest x1 1.33 us: carried_state(): back = lax.all_to_all(summed, 'inner', 0, 0, tiled=True)]
    add x0 -> x1, other arithmetic: none -> 0.83 us  [carried_state(): summed = inner_before + outer_chunk.reshape(1, -1, lanes)]
  transfers between devices with their start and end apart: 1 -> 2, of which waited for: 1 -> 2; matrix products, arithmetic and copies ran while one was open for 0% -> 0% of each run, Pallas kernels for 9% -> 9%
where the time goes in v6:
time: 82.4 us; the launch traced here: 82 us
  blocking collectives  34.9 us (42%)
  Pallas kernels  22.5 us (27%)
  starting transfers between devices  10.8 us (13%)
  waiting for transfers between devices  10.8 us (13%)
  local copies, waits for them, and re-layouts  1.53 us (2%)
  other arithmetic  1.31 us (2%)
    all_to_all x1, blocking collectives, carried_state(): lax.all_to_all(group_total.reshape(n_outer, -1, lanes), 'outer', 0, 0, ti...  19 us
    all_to_all x1, blocking collectives, carried_state(): gathered = lax.all_to_all(chunks, 'inner', 0, 0, tiled=False)  15.9 us
    pallas_call x1, Pallas kernels, layer(): pl.pallas_call(layer_kernel, out_shape=jax.ShapeDtypeStruct((rows, out_wi...  11.6 us
    all_to_all x1, waiting for transfers between devices, carried_state(): outer_chunk = lax.all_to_all(outer_before, 'outer', 0, 0, tiled=False)  8.83 us
    pallas_call x1, Pallas kernels, intra_block(): pl.pallas_call(intra_kernel, out_shape=(jax.ShapeDtypeStruct((rows, width...  7.44 us
    all_to_all x1, starting transfers between devices, carried_state(): back = lax.all_to_all(summed, 'inner', 0, 0, tiled=False)  6.97 us
    all_to_all x1, starting transfers between devices, carried_state(): outer_chunk = lax.all_to_all(outer_before, 'outer', 0, 0, tiled=False)  3.85 us
    pallas_call x1, Pallas kernels, state_totals(): pl.pallas_call(state_kernel, out_shape=jax.ShapeDtypeStruct((H, DH, DH),...  3.49 us
  transfers between devices with their start and end apart: 2, of which 2 were waited for; matrix products, arithmetic and copies ran while one was open for 0% of the time, Pallas kernels for 9%

profile of v6, /device:TPU:1, one launch (start us, length us, event | category | flops | bytes accessed | tf_op | source)
XLA Modules:
  0.0 82.0 jit_solution(18192107138022120801)
XLA Ops:
  0.0 3.5 %shard_map.56 = f32[8,128,128]{2,1,0:T(8,128)} custom-call(bf16[1024,1024]{1,0:T(8,128)(2,1)} %k_ref.3, bf16[1024,1024]{1,0:T(8,128)(2,1)} %v_ref.3), custom_call_target="tpu_custom_call" | custom-call | tf_op jit(solution)/shard_map/pallas_call | solution.py:54
  3.5 15.9 %all_to_all.20 = f32[8,128,128]{2,1,0:T(8,128)S(1)} all-to-all(f32[8,128,128]{2,1,0:T(8,128)} %shard_map.56), channel_id=1, replica_groups=mesh['outer'=32,'inner'=8] {'inner'}, dimensions={0} | all-to-all | bytes 1048576 | tf_op jit(solution)/shard_map/all_to_all | solution.py:23
  19.4 0.4 fusion
  19.9 19.0 %all_to_all.21 = f32[32,4,128]{2,1,0:T(4,128)S(1)} all-to-all(f32[32,4,128]{2,1,0:T(4,128)S(1)} %bitcast.6), channel_id=1, replica_groups=mesh['outer'=32,'inner'=8] {'outer'}, dimensions={0} | all-to-all | bytes 131072 | tf_op jit(solution)/shard_map/all_to_all | solution.py:25
  38.9 0.6 concatenate.7
  39.6 3.9 %all-to-all-start.2 = ((f32[32,4,128]{2,1,0:T(4,128)}), f32[32,4,128]{2,1,0:T(4,128)S(1)}, u32[]{:S(2)}, u32[]{:S(2)}) async-start(f32[32,4,128]{2,1,0:T(4,128)} %concatenate.7), calls=%async_computation.2 | async-start | bytes 131072 | tf_op jit(solution)/shard_map/all_to_all | solution.py:27
  43.5 8.8 %all-to-all-done.2 = f32[32,4,128]{2,1,0:T(4,128)S(1)} async-done(((f32[32,4,128]{2,1,0:T(4,128)}), f32[32,4,128]{2,1,0:T(4,128)S(1)}, u32[]{:S(2)}, u32[]{:S(2)}) %all-to-all-start.2) | async-done | bytes 65568 | tf_op jit(solution)/shard_map/all_to_all | solution.py:27
  52.3 0.8 %pad_add_fusion = f32[8,128,128]{2,1,0:T(8,128)} fusion(f32[7,128,128]{2,1,0:T(8,128)S(1)} %slice.12, f32[128,128]{1,0:T(8,128)S(1)} %bitcast.5), kind=kLoop, calls=%fused_computation | loop fusion | flops 131072 | bytes 1048576 | tf_op jit(solution)/shard_map/add | solution.py:28
  53.2 7.0 %all-to-all-start.3 = ((f32[8,128,128]{2,1,0:T(8,128)}), f32[8,128,128]{2,1,0:T(8,128)S(1)}, u32[]{:S(2)}, u32[]{:S(2)}) async-start(f32[8,128,128]{2,1,0:T(8,128)} %pad_add_fusion), calls=%async_computation.3 | async-start | bytes 1048576 | tf_op jit(solution)/shard_map/all_to_all | solution.py:29
  60.1 7.4 %shard_map.55 = (f32[1024,1024]{1,0:T(8,128)}, f32[8,8,128,128]{3,2,1,0:T(8,128)}) custom-call(bf16[1024,1024]{1,0:T(8,128)(2,1)} %q_ref.3, bf16[1024,1024]{1,0:T(8,128)(2,1)} %k_ref.3, bf16[1024,1024]{1,0:T(8,128)(2,1)} %v_ref.3), custom_call_target="tpu_custom_call" | custom-call | tf_op jit(solution)/shard_map/pallas_call | solution.py:102
  67.6 1.9 %all-to-all-done.3.c_ref = f32[8,128,128]{2,1,0:T(8,128)S(1)} async-done(((f32[8,128,128]{2,1,0:T(8,128)}), f32[8,128,128]{2,1,0:T(8,128)S(1)}, u32[]{:S(2)}, u32[]{:S(2)}) %all-to-all-start.3) | async-done | bytes 524320 | tf_op jit(solution)/shard_map/all_to_all | solution.py:29
  69.5 0.0 copy-start
  69.5 0.8 %copy-done = f32[8,128,128]{2,1,0:T(8,128)} copy-done((f32[8,128,128]{2,1,0:T(8,128)}, f32[8,128,128]{2,1,0:T(8,128)S(1)}, u32[]{:S(2)}) %copy-start) | copy-done | bytes 524312
  70.4 11.6 %shard_map.57 = bf16[1024,2048]{1,0:T(8,128)(2,1)} custom-call(bf16[1024,1024]{1,0:T(8,128)(2,1)} %q_ref.3, f32[1024,1024]{1,0:T(8,128)} %get-tuple-element.7.i_ref, f32[8,8,128,128]{3,2,1,0:T(8,128)} %get-tuple-element.8.w_in_ref, f32[8,128,128]{2,1,0:T(8,128)} %copy-done, f32[1,1024]{1,0:T(1,128)} %bitcast.7, bf16[1024,2048]{1,0:T(8,128)(2,1)} %w_ref.1), custom_call_target="tpu_custom_call" | custom-call | tf_op jit(solution)/shard_map/pallas_call | solution.py:140
  (4 shorter events, 0.1 us)
Async XLA Ops:
  39.6 12.7 %all-to-all-start.2 = ((f32[32,4,128]{2,1,0:T(4,128)}), f32[32,4,128]{2,1,0:T(4,128)S(1)}, u32[]{:S(2)}, u32[]{:S(2)}) async-start(f32[32,4,128]{2,1,0:T(4,128)} %concatenate.7), calls=%async_computation.2 | async-start | bytes 131072 | tf_op jit(solution)/shard_map/all_to_all | solution.py:27
  53.2 16.4 %all-to-all-start.3 = ((f32[8,128,128]{2,1,0:T(8,128)}), f32[8,128,128]{2,1,0:T(8,128)S(1)}, u32[]{:S(2)}, u32[]{:S(2)}) async-start(f32[8,128,128]{2,1,0:T(8,128)} %pad_add_fusion), calls=%async_computation.3 | async-start | bytes 1048576 | tf_op jit(solution)/shard_map/all_to_all | solution.py:29
  69.5 0.8 %copy-start = (f32[8,128,128]{2,1,0:T(8,128)}, f32[8,128,128]{2,1,0:T(8,128)S(1)}, u32[]{:S(2)}) copy-start(f32[8,128,128]{2,1,0:T(8,128)S(1)} %all-to-all-done.3.c_ref) | copy-start | bytes 1572868

commit v7 on v6

--- a/solution.py
+++ b/solution.py
@@ -116,7 +116,22 @@
     )(queries, keys, values)
 
 
-def layer_kernel(q_ref, i_ref, w_in_ref, c_ref, g_ref, w_ref, o_ref, n_ref):
+WEIGHT_PARTS = 4
+
+
+def layer_kernel(q_ref, i_ref, w_in_ref, c_ref, g_ref, w_hbm, o_ref, n_ref, w_ref, sems):
+    first = pl.program_id(0) == 0
+    rows_part = w_ref.shape[0] // WEIGHT_PARTS
+
+    def weight_copy(j):
+        part = pl.ds(j * rows_part, rows_part)
+        return pltpu.make_async_copy(w_hbm.at[part, :], w_ref.at[part, :], sems.at[j])
+
+    @pl.when(first)
+    def _():
+        for j in range(WEIGHT_PARTS):
+            weight_copy(j).start()
+
     for b in range(TILE // C):
         rows = slice(b * C, (b + 1) * C)
         for h in range(H):
@@ -127,9 +142,16 @@
             mean_square = jnp.mean(attended * attended, axis=-1, keepdims=True)
             normed = attended * lax.rsqrt(mean_square + 1e-06) * g_ref[:, cols]
             n_ref[rows, cols] = normed.astype(jnp.bfloat16)
-    o_ref[...] = jnp.dot(n_ref[...], w_ref[...], preferred_element_type=jnp.float32).astype(
-        jnp.bfloat16
-    )
+    total = None
+    for j in range(WEIGHT_PARTS):
+        @pl.when(first)
+        def _():
+            weight_copy(j).wait()
+
+        part = slice(j * rows_part, (j + 1) * rows_part)
+        piece = jnp.dot(n_ref[:, part], w_ref[part, :], preferred_element_type=jnp.float32)
+        total = piece if total is None else total + piece
+    o_ref[...] = total.astype(jnp.bfloat16)
 
 
 def layer(queries, inside, within, carried, norm_gain, out_weight):
@@ -147,10 +169,15 @@
             pl.BlockSpec((TILE // C, H, DH, DH), lambda t: (t, 0, 0, 0)),
             pl.BlockSpec((H, DH, DH), lambda t: (0, 0, 0)),
             pl.BlockSpec((1, width), fixed2),
-            pl.BlockSpec((width, out_width), fixed2),
+            pl.BlockSpec(memory_space=pl.ANY),
         ],
         out_specs=pl.BlockSpec((TILE, out_width), tok),
-        scratch_shapes=[pltpu.VMEM((TILE, width), jnp.bfloat16)],
+        scratch_shapes=[
+            pltpu.VMEM((TILE, width), jnp.bfloat16),
+            pltpu.VMEM((width, out_width), jnp.bfloat16),
+            pltpu.SemaphoreType.DMA((WEIGHT_PARTS,)),
+        ],
+        compiler_params=pltpu.CompilerParams(dimension_semantics=("arbitrary",)),
     )(queries, inside, within, carried, norm_gain.reshape(1, width), out_weight)
 
 

time: 82.4 us -> 83 us (level)
  no operation moved by 1% of the time
where the time goes in v7:
time: 83 us; the launch traced here: 82.6 us
  blocking collectives  34.9 us (42%)
  Pallas kernels  23.1 us (28%)
  starting transfers between devices  10.8 us (13%)
  waiting for transfers between devices  10.8 us (13%)
  local copies, waits for them, and re-layouts  1.53 us (2%)
  other arithmetic  1.31 us (2%)
    all_to_all x1, blocking collectives, carried_state(): lax.all_to_all(group_total.reshape(n_outer, -1, lanes), 'outer', 0, 0, ti...  19 us
    all_to_all x1, blocking collectives, carried_state(): gathered = lax.all_to_all(chunks, 'inner', 0, 0, tiled=False)  15.9 us
    pallas_call x1, Pallas kernels, layer(): pl.pallas_call(layer_kernel, out_shape=jax.ShapeDtypeStruct((rows, out_wi...  12.2 us
    all_to_all x1, waiting for transfers between devices, carried_state(): outer_chunk = lax.all_to_all(outer_before, 'outer', 0, 0, tiled=False)  8.83 us
    pallas_call x1, Pallas kernels, intra_block(): pl.pallas_call(intra_kernel, out_shape=(jax.ShapeDtypeStruct((rows, width...  7.44 us
    all_to_all x1, starting transfers between devices, carried_state(): back = lax.all_to_all(summed, 'inner', 0, 0, tiled=False)  6.97 us
    all_to_all x1, starting transfers between devices, carried_state(): outer_chunk = lax.all_to_all(outer_before, 'outer', 0, 0, tiled=False)  3.85 us
    pallas_call x1, Pallas kernels, state_totals(): pl.pallas_call(state_kernel, out_shape=jax.ShapeDtypeStruct((H, DH, DH),...  3.49 us
  transfers between devices with their start and end apart: 2, of which 2 were waited for; matrix products, arithmetic and copies ran while one was open for 0% of the time, Pallas kernels for 9%

profile of v7, /device:TPU:1, one launch (start us, length us, event | category | flops | bytes accessed | tf_op | source)
XLA Modules:
  0.0 82.6 jit_solution(12965913389480210403)
XLA Ops:
  0.0 3.5 %shard_map.56 = f32[8,128,128]{2,1,0:T(8,128)} custom-call(bf16[1024,1024]{1,0:T(8,128)(2,1)} %k_ref.3, bf16[1024,1024]{1,0:T(8,128)(2,1)} %v_ref.3), custom_call_target="tpu_custom_call" | custom-call | tf_op jit(solution)/shard_map/pallas_call | solution.py:54
  3.5 15.9 %all_to_all.20 = f32[8,128,128]{2,1,0:T(8,128)S(1)} all-to-all(f32[8,128,128]{2,1,0:T(8,128)} %shard_map.56), channel_id=1, replica_groups=mesh['outer'=32,'inner'=8] {'inner'}, dimensions={0} | all-to-all | bytes 1048576 | tf_op jit(solution)/shard_map/all_to_all | solution.py:23
  19.4 0.4 fusion
  19.9 19.0 %all_to_all.21 = f32[32,4,128]{2,1,0:T(4,128)S(1)} all-to-all(f32[32,4,128]{2,1,0:T(4,128)S(1)} %bitcast.6), channel_id=1, replica_groups=mesh['outer'=32,'inner'=8] {'outer'}, dimensions={0} | all-to-all | bytes 131072 | tf_op jit(solution)/shard_map/all_to_all | solution.py:25
  38.9 0.6 concatenate.7
  39.6 3.9 %all-to-all-start.2 = ((f32[32,4,128]{2,1,0:T(4,128)}), f32[32,4,128]{2,1,0:T(4,128)S(1)}, u32[]{:S(2)}, u32[]{:S(2)}) async-start(f32[32,4,128]{2,1,0:T(4,128)} %concatenate.7), calls=%async_computation.2 | async-start | bytes 131072 | tf_op jit(solution)/shard_map/all_to_all | solution.py:27
  43.5 8.8 %all-to-all-done.2 = f32[32,4,128]{2,1,0:T(4,128)S(1)} async-done(((f32[32,4,128]{2,1,0:T(4,128)}), f32[32,4,128]{2,1,0:T(4,128)S(1)}, u32[]{:S(2)}, u32[]{:S(2)}) %all-to-all-start.2) | async-done | bytes 65568 | tf_op jit(solution)/shard_map/all_to_all | solution.py:27
  52.3 0.8 %pad_add_fusion = f32[8,128,128]{2,1,0:T(8,128)} fusion(f32[7,128,128]{2,1,0:T(8,128)S(1)} %slice.12, f32[128,128]{1,0:T(8,128)S(1)} %bitcast.5), kind=kLoop, calls=%fused_computation | loop fusion | flops 131072 | bytes 1048576 | tf_op jit(solution)/shard_map/add | solution.py:28
  53.2 7.0 %all-to-all-start.3 = ((f32[8,128,128]{2,1,0:T(8,128)}), f32[8,128,128]{2,1,0:T(8,128)S(1)}, u32[]{:S(2)}, u32[]{:S(2)}) async-start(f32[8,128,128]{2,1,0:T(8,128)} %pad_add_fusion), calls=%async_computation.3 | async-start | bytes 1048576 | tf_op jit(solution)/shard_map/all_to_all | solution.py:29
  60.1 7.4 %shard_map.55 = (f32[1024,1024]{1,0:T(8,128)}, f32[8,8,128,128]{3,2,1,0:T(8,128)}) custom-call(bf16[1024,1024]{1,0:T(8,128)(2,1)} %q_ref.3, bf16[1024,1024]{1,0:T(8,128)(2,1)} %k_ref.3, bf16[1024,1024]{1,0:T(8,128)(2,1)} %v_ref.3), custom_call_target="tpu_custom_call" | custom-call | tf_op jit(solution)/shard_map/pallas_call | solution.py:102
  67.6 1.9 %all-to-all-done.3.c_ref = f32[8,128,128]{2,1,0:T(8,128)S(1)} async-done(((f32[8,128,128]{2,1,0:T(8,128)}), f32[8,128,128]{2,1,0:T(8,128)S(1)}, u32[]{:S(2)}, u32[]{:S(2)}) %all-to-all-start.3) | async-done | bytes 524320 | tf_op jit(solution)/shard_map/all_to_all | solution.py:29
  69.5 0.0 copy-start
  69.5 0.8 %copy-done = f32[8,128,128]{2,1,0:T(8,128)} copy-done((f32[8,128,128]{2,1,0:T(8,128)}, f32[8,128,128]{2,1,0:T(8,128)S(1)}, u32[]{:S(2)}) %copy-start) | copy-done | bytes 524312
  70.4 12.2 %shard_map.57 = bf16[1024,2048]{1,0:T(8,128)(2,1)} custom-call(bf16[1024,1024]{1,0:T(8,128)(2,1)} %q_ref.3, f32[1024,1024]{1,0:T(8,128)} %get-tuple-element.7.i_ref, f32[8,8,128,128]{3,2,1,0:T(8,128)} %get-tuple-element.8.w_in_ref, f32[8,128,128]{2,1,0:T(8,128)} %copy-done, f32[1,1024]{1,0:T(1,128)} %bitcast.7, bf16[1024,2048]{1,0:T(8,128)(2,1)} %w_hbm.1), custom_call_target="tpu_custom_call" | custom-call | tf_op jit(solution)/shard_map/pallas_call | solution.py:162
  (4 shorter events, 0.1 us)
Async XLA Ops:
  39.6 12.7 %all-to-all-start.2 = ((f32[32,4,128]{2,1,0:T(4,128)}), f32[32,4,128]{2,1,0:T(4,128)S(1)}, u32[]{:S(2)}, u32[]{:S(2)}) async-start(f32[32,4,128]{2,1,0:T(4,128)} %concatenate.7), calls=%async_computation.2 | async-start | bytes 131072 | tf_op jit(solution)/shard_map/all_to_all | solution.py:27
  53.2 16.4 %all-to-all-start.3 = ((f32[8,128,128]{2,1,0:T(8,128)}), f32[8,128,128]{2,1,0:T(8,128)S(1)}, u32[]{:S(2)}, u32[]{:S(2)}) async-start(f32[8,128,128]{2,1,0:T(8,128)} %pad_add_fusion), calls=%async_computation.3 | async-start | bytes 1048576 | tf_op jit(solution)/shard_map/all_to_all | solution.py:29
  69.5 0.8 %copy-start = (f32[8,128,128]{2,1,0:T(8,128)}, f32[8,128,128]{2,1,0:T(8,128)S(1)}, u32[]{:S(2)}) copy-start(f32[8,128,128]{2,1,0:T(8,128)S(1)} %all-to-all-done.3.c_ref) | copy-start | bytes 1572868

commit v8 on v6

--- a/solution.py
+++ b/solution.py
@@ -16,17 +16,18 @@
 
 
 def carried_state(local_total):
+    axes = ("outer", "inner")
+    devices = lax.axis_size(axes)
+    lanes = local_total.shape[-1]
+    pieces = local_total.reshape(devices, -1, lanes)
+    gathered = lax.all_to_all(pieces, axes, 0, 0, tiled=False)
     n_inner = lax.axis_size("inner")
-    n_outer = lax.axis_size("outer")
-    lanes = local_total.shape[-1]
-    chunks = local_total.reshape(n_inner, -1, lanes)
-    gathered = lax.all_to_all(chunks, "inner", 0, 0, tiled=False)
-    inner_before, group_total = exclusive_cumsum(gathered)
-    pieces = lax.all_to_all(group_total.reshape(n_outer, -1, lanes), "outer", 0, 0, tiled=False)
-    outer_before, _ = exclusive_cumsum(pieces)
-    outer_chunk = lax.all_to_all(outer_before, "outer", 0, 0, tiled=False)
-    summed = inner_before + outer_chunk.reshape(1, -1, lanes)
-    back = lax.all_to_all(summed, "inner", 0, 0, tiled=False)
+    groups = gathered.reshape(devices // n_inner, n_inner, -1, lanes)
+    running = jnp.cumsum(groups, axis=1)
+    inner_before = jnp.concatenate([jnp.zeros_like(running[:, :1]), running[:, :-1]], axis=1)
+    outer_before, _ = exclusive_cumsum(running[:, -1])
+    before = (inner_before + outer_before[:, None]).reshape(gathered.shape)
+    back = lax.all_to_all(before, axes, 0, 0, tiled=False)
     return back.reshape(local_total.shape)
 
 

time: 82.4 us -> 79.8 us (0.968)
  starting transfers between devices: 10.8 us -> 6.13 us
  waiting for transfers between devices: 10.8 us -> 12.5 us
    all_to_all x2 -> x1, starting transfers between devices: 10.8 us -> 6.13 us  [carried_state(): back = lax.all_to_all(before, axes, 0, 0, tiled=False)]
    all_to_all x2 -> x1, waiting for transfers between devices: 10.8 us -> 12.5 us  [carried_state(): back = lax.all_to_all(before, axes, 0, 0, tiled=False)]
    reshape x0 -> x1, local copies, waits for them, and re-layouts: none -> 1.13 us  [carried_state(): before = (inner_before + outer_before[:, None]).reshape(gathered.shape)]
    add x1 -> x0, other arithmetic: 0.83 us -> none  [carried_state(): summed = inner_before + outer_chunk.reshape(1, -1, lanes)]
    all_to_all x2 -> x1, blocking collectives: 34.9 us -> 35.6 us  [carried_state(): gathered = lax.all_to_all(pieces, axes, 0, 0, tiled=False)]
  transfers between devices with their start and end apart: 2 -> 1, of which waited for: 2 -> 1; matrix products, arithmetic and copies ran while one was open for 0% -> 0% of each run, Pallas kernels for 9% -> 9%
where the time goes in v8:
time: 79.8 us; the launch traced here: 79.5 us
  blocking collectives  35.6 us (45%)
  Pallas kernels  22.6 us (28%)
  waiting for transfers between devices  12.5 us (16%)
  starting transfers between devices  6.13 us (8%)
  local copies, waits for them, and re-layouts  2.1 us (3%)
    all_to_all x1, blocking collectives, carried_state(): gathered = lax.all_to_all(pieces, axes, 0, 0, tiled=False)  35.6 us
    all_to_all x1, waiting for transfers between devices, carried_state(): back = lax.all_to_all(before, axes, 0, 0, tiled=False)  12.5 us
    pallas_call x1, Pallas kernels, layer(): pl.pallas_call(layer_kernel, out_shape=jax.ShapeDtypeStruct((rows, out_wi...  11.6 us
    pallas_call x1, Pallas kernels, intra_block(): pl.pallas_call(intra_kernel, out_shape=(jax.ShapeDtypeStruct((rows, width...  7.45 us
    all_to_all x1, starting transfers between devices, carried_state(): back = lax.all_to_all(before, axes, 0, 0, tiled=False)  6.13 us
    pallas_call x1, Pallas kernels, state_totals(): pl.pallas_call(state_kernel, out_shape=jax.ShapeDtypeStruct((H, DH, DH),...  3.49 us
  transfers between devices with their start and end apart: 1, of which 1 were waited for; matrix products, arithmetic and copies ran while one was open for 0% of the time, Pallas kernels for 9%

profile of v8, /device:TPU:1, one launch (start us, length us, event | category | flops | bytes accessed | tf_op | source)
XLA Modules:
  0.0 79.5 jit_solution(11752472837024572832)
XLA Ops:
  0.0 3.5 %shard_map.56 = f32[8,128,128]{2,1,0:T(8,128)} custom-call(bf16[1024,1024]{1,0:T(8,128)(2,1)} %k_ref.3, bf16[1024,1024]{1,0:T(8,128)(2,1)} %v_ref.3), custom_call_target="tpu_custom_call" | custom-call | tf_op jit(solution)/shard_map/pallas_call | solution.py:55
  3.5 35.6 %all_to_all.10 = f32[256,4,128]{2,1,0:T(4,128)S(1)} all-to-all(f32[256,4,128]{2,1,0:T(4,128)} %bitcast.11), channel_id=1, replica_groups=mesh['outer'=32,'inner'=8] {'outer','inner'}, dimensions={0} | all-to-all | bytes 1048576 | tf_op jit(solution)/shard_map/all_to_all | solution.py:23
  39.1 0.5 reduce_window_sum.22
  39.6 0.1 slice.13
  39.8 0.1 add_bitcast_fusion
  39.9 1.1 %copy.13 = f32[256,4,128]{2,1,0:T(4,128)} copy(f32[256,4,128]{2,0,1:T(8,128)S(1)} %add_bitcast_fusion) | data formatting | bytes 1048576 | tf_op jit(solution)/shard_map/reshape | solution.py:29
  41.0 6.1 %all-to-all-start.1 = ((f32[256,4,128]{2,1,0:T(4,128)}), f32[256,4,128]{2,1,0:T(4,128)S(1)}, u32[]{:S(2)}, u32[]{:S(2)}) async-start(f32[256,4,128]{2,1,0:T(4,128)} %copy.13), calls=%async_computation.1 | async-start | bytes 1048576 | tf_op jit(solution)/shard_map/all_to_all | solution.py:30
  47.1 7.5 %shard_map.55 = (f32[1024,1024]{1,0:T(8,128)}, f32[8,8,128,128]{3,2,1,0:T(8,128)}) custom-call(bf16[1024,1024]{1,0:T(8,128)(2,1)} %q_ref.3, bf16[1024,1024]{1,0:T(8,128)(2,1)} %k_ref.3, bf16[1024,1024]{1,0:T(8,128)(2,1)} %v_ref.3), custom_call_target="tpu_custom_call" | custom-call | tf_op jit(solution)/shard_map/pallas_call | solution.py:103
  54.6 12.5 %all-to-all-done.1 = f32[256,4,128]{2,1,0:T(4,128)S(1)} async-done(((f32[256,4,128]{2,1,0:T(4,128)}), f32[256,4,128]{2,1,0:T(4,128)S(1)}, u32[]{:S(2)}, u32[]{:S(2)}) %all-to-all-start.1) | async-done | bytes 524320 | tf_op jit(solution)/shard_map/all_to_all | solution.py:30
  67.1 0.0 copy-start
  67.1 0.8 %copy-done = f32[256,4,128]{2,1,0:T(4,128)} copy-done((f32[256,4,128]{2,1,0:T(4,128)}, f32[256,4,128]{2,1,0:T(4,128)S(1)}, u32[]{:S(2)}) %copy-start) | copy-done | bytes 524312
  67.9 11.6 %shard_map.57 = bf16[1024,2048]{1,0:T(8,128)(2,1)} custom-call(bf16[1024,1024]{1,0:T(8,128)(2,1)} %q_ref.3, f32[1024,1024]{1,0:T(8,128)} %get-tuple-element.7.i_ref, f32[8,8,128,128]{3,2,1,0:T(8,128)} %get-tuple-element.8.w_in_ref, f32[8,128,128]{2,1,0:T(8,128)} %bitcast.13, f32[1,1024]{1,0:T(1,128)} %bitcast.15, bf16[1024,2048]{1,0:T(8,128)(2,1)} %w_ref.1), custom_call_target="tpu_custom_call" | custom-call | tf_op jit(solution)/shard_map/pallas_call | solution.py:141
  (5 shorter events, 0.1 us)
Async XLA Ops:
  41.0 26.1 %all-to-all-start.1 = ((f32[256,4,128]{2,1,0:T(4,128)}), f32[256,4,128]{2,1,0:T(4,128)S(1)}, u32[]{:S(2)}, u32[]{:S(2)}) async-start(f32[256,4,128]{2,1,0:T(4,128)} %copy.13), calls=%async_computation.1 | async-start | bytes 1048576 | tf_op jit(solution)/shard_map/all_to_all | solution.py:30
  67.1 0.8 %copy-start = (f32[256,4,128]{2,1,0:T(4,128)}, f32[256,4,128]{2,1,0:T(4,128)S(1)}, u32[]{:S(2)}) copy-start(f32[256,4,128]{2,1,0:T(4,128)S(1)} %all-to-all-done.1) | copy-start | bytes 1572868

commit v9 on v8

--- a/solution.py
+++ b/solution.py
@@ -21,12 +21,13 @@
     lanes = local_total.shape[-1]
     pieces = local_total.reshape(devices, -1, lanes)
     gathered = lax.all_to_all(pieces, axes, 0, 0, tiled=False)
-    n_inner = lax.axis_size("inner")
-    groups = gathered.reshape(devices // n_inner, n_inner, -1, lanes)
-    running = jnp.cumsum(groups, axis=1)
-    inner_before = jnp.concatenate([jnp.zeros_like(running[:, :1]), running[:, :-1]], axis=1)
-    outer_before, _ = exclusive_cumsum(running[:, -1])
-    before = (inner_before + outer_before[:, None]).reshape(gathered.shape)
+    earlier = lax.broadcasted_iota(jnp.int32, (devices, devices), 0) > lax.broadcasted_iota(
+        jnp.int32, (devices, devices), 1
+    )
+    before = jnp.dot(
+        earlier.astype(jnp.float32), gathered.reshape(devices, -1),
+        precision=lax.Precision.HIGHEST, preferred_element_type=jnp.float32,
+    ).reshape(gathered.shape)
     back = lax.all_to_all(before, axes, 0, 0, tiled=False)
     return back.reshape(local_total.shape)
 

time: 79.8 us -> 79.7 us (level)
    dot_general x0 -> x1, local copies, waits for them, and re-layouts: none -> 1.13 us  [carried_state(): jnp.dot(earlier.astype(jnp.float32), gathered.reshape(devices, -1), preci...]
    reshape x1, local copies, waits for them, and re-layouts: 1.13 us -> 0.22 us  [carried_state(): gathered.reshape(devices, -1)]
where the time goes in v9:
time: 79.7 us; the launch traced here: 79.4 us
  blocking collectives  35.6 us (45%)
  Pallas kernels  22.6 us (28%)
  waiting for transfers between devices  12.5 us (16%)
  starting transfers between devices  6.13 us (8%)
  local copies, waits for them, and re-layouts  2.18 us (3%)
    all_to_all x1, blocking collectives, carried_state(): gathered = lax.all_to_all(pieces, axes, 0, 0, tiled=False)  35.6 us
    all_to_all x1, waiting for transfers between devices, carried_state(): back = lax.all_to_all(before, axes, 0, 0, tiled=False)  12.5 us
    pallas_call x1, Pallas kernels, layer(): pl.pallas_call(layer_kernel, out_shape=jax.ShapeDtypeStruct((rows, out_wi...  11.6 us
    pallas_call x1, Pallas kernels, intra_block(): pl.pallas_call(intra_kernel, out_shape=(jax.ShapeDtypeStruct((rows, width...  7.46 us
    all_to_all x1, starting transfers between devices, carried_state(): back = lax.all_to_all(before, axes, 0, 0, tiled=False)  6.13 us
    pallas_call x1, Pallas kernels, state_totals(): pl.pallas_call(state_kernel, out_shape=jax.ShapeDtypeStruct((H, DH, DH),...  3.49 us
  transfers between devices with their start and end apart: 1, of which 1 were waited for; matrix products, arithmetic and copies ran while one was open for 0% of the time, Pallas kernels for 9%

profile of v9, /device:TPU:1, one launch (start us, length us, event | category | flops | bytes accessed | tf_op | source)
XLA Modules:
  0.0 79.4 jit_solution(14943351506349933907)
XLA Ops:
  0.0 3.5 %shard_map.56 = f32[8,128,128]{2,1,0:T(8,128)} custom-call(bf16[1024,1024]{1,0:T(8,128)(2,1)} %k_ref.3, bf16[1024,1024]{1,0:T(8,128)(2,1)} %v_ref.3), custom_call_target="tpu_custom_call" | custom-call | tf_op jit(solution)/shard_map/pallas_call | solution.py:56
  3.5 35.6 %all_to_all.10 = f32[256,4,128]{2,1,0:T(4,128)S(1)} all-to-all(f32[256,4,128]{2,1,0:T(4,128)} %bitcast.13), channel_id=1, replica_groups=mesh['outer'=32,'inner'=8] {'outer','inner'}, dimensions={0} | all-to-all | bytes 1048576 | tf_op jit(solution)/shard_map/all_to_all | solution.py:23
  39.1 0.2 copy.10
  39.3 0.4 fusion
  39.8 1.1 %copy.9 = f32[256,4,128]{2,1,0:T(4,128)} copy(f32[256,4,128]{2,0,1:T(8,128)S(1)} %fusion) | data formatting | bytes 1048576 | tf_op jit(solution)/shard_map/dot_general | solution.py:27
  40.9 6.1 %all-to-all-start.1 = ((f32[256,4,128]{2,1,0:T(4,128)}), f32[256,4,128]{2,1,0:T(4,128)S(1)}, u32[]{:S(2)}, u32[]{:S(2)}) async-start(f32[256,4,128]{2,1,0:T(4,128)} %copy.9), calls=%async_computation.1 | async-start | bytes 1048576 | tf_op jit(solution)/shard_map/all_to_all | solution.py:31
  47.0 7.5 %shard_map.55 = (f32[1024,1024]{1,0:T(8,128)}, f32[8,8,128,128]{3,2,1,0:T(8,128)}) custom-call(bf16[1024,1024]{1,0:T(8,128)(2,1)} %q_ref.3, bf16[1024,1024]{1,0:T(8,128)(2,1)} %k_ref.3, bf16[1024,1024]{1,0:T(8,128)(2,1)} %v_ref.3), custom_call_target="tpu_custom_call" | custom-call | tf_op jit(solution)/shard_map/pallas_call | solution.py:104
  54.5 12.5 %all-to-all-done.1 = f32[256,4,128]{2,1,0:T(4,128)S(1)} async-done(((f32[256,4,128]{2,1,0:T(4,128)}), f32[256,4,128]{2,1,0:T(4,128)S(1)}, u32[]{:S(2)}, u32[]{:S(2)}) %all-to-all-start.1) | async-done | bytes 524320 | tf_op jit(solution)/shard_map/all_to_all | solution.py:31
  67.0 0.0 copy-start
  67.0 0.8 %copy-done = f32[256,4,128]{2,1,0:T(4,128)} copy-done((f32[256,4,128]{2,1,0:T(4,128)}, f32[256,4,128]{2,1,0:T(4,128)S(1)}, u32[]{:S(2)}) %copy-start) | copy-done | bytes 524312
  67.8 11.6 %shard_map.57 = bf16[1024,2048]{1,0:T(8,128)(2,1)} custom-call(bf16[1024,1024]{1,0:T(8,128)(2,1)} %q_ref.3, f32[1024,1024]{1,0:T(8,128)} %get-tuple-element.7.i_ref, f32[8,8,128,128]{3,2,1,0:T(8,128)} %get-tuple-element.8.w_in_ref, f32[8,128,128]{2,1,0:T(8,128)} %bitcast.14, f32[1,1024]{1,0:T(1,128)} %bitcast.15, bf16[1024,2048]{1,0:T(8,128)(2,1)} %w_ref.1), custom_call_target="tpu_custom_call" | custom-call | tf_op jit(solution)/shard_map/pallas_call | solution.py:142
Async XLA Ops:
  40.9 26.1 %all-to-all-start.1 = ((f32[256,4,128]{2,1,0:T(4,128)}), f32[256,4,128]{2,1,0:T(4,128)S(1)}, u32[]{:S(2)}, u32[]{:S(2)}) async-start(f32[256,4,128]{2,1,0:T(4,128)} %copy.9), calls=%async_computation.1 | async-start | bytes 1048576 | tf_op jit(solution)/shard_map/all_to_all | solution.py:31
  67.0 0.8 %copy-start = (f32[256,4,128]{2,1,0:T(4,128)}, f32[256,4,128]{2,1,0:T(4,128)S(1)}, u32[]{:S(2)}) copy-start(f32[256,4,128]{2,1,0:T(4,128)S(1)} %all-to-all-done.1) | copy-start | bytes 1572868

commit v10 on v9

--- a/solution.py
+++ b/solution.py
@@ -15,7 +15,7 @@
     return jnp.concatenate([jnp.zeros_like(rows[:1]), running[:-1]], axis=0), running[-1]
 
 
-def carried_state(local_total):
+def carried_state(local_total, held):
     axes = ("outer", "inner")
     devices = lax.axis_size(axes)
     lanes = local_total.shape[-1]
@@ -28,8 +28,9 @@
         earlier.astype(jnp.float32), gathered.reshape(devices, -1),
         precision=lax.Precision.HIGHEST, preferred_element_type=jnp.float32,
     ).reshape(gathered.shape)
+    before, held = lax.optimization_barrier((before, held))
     back = lax.all_to_all(before, axes, 0, 0, tiled=False)
-    return back.reshape(local_total.shape)
+    return back.reshape(local_total.shape), held
 
 
 TILE = 256
@@ -158,8 +159,7 @@
 
 def on_device(queries, keys, values, norm_gain, out_weight):
     local_total = state_totals(keys, values)
-    inside, within = intra_block(queries, keys, values)
-    carried = carried_state(local_total)
+    carried, (inside, within) = carried_state(local_total, intra_block(queries, keys, values))
     return layer(queries, inside, within, carried, norm_gain, out_weight)
 
 

time: 79.7 us -> 78.3 us (0.982)
  starting transfers between devices: 6.13 us -> 15.6 us
  blocking collectives: 35.6 us -> 26.3 us
  local copies, waits for them, and re-layouts: 2.18 us -> 0.56 us
    all_to_all x1, starting transfers between devices: 6.13 us -> 15.6 us  [carried_state(): gathered = lax.all_to_all(pieces, axes, 0, 0, tiled=False)]
    all_to_all x1, blocking collectives: 35.6 us -> 26.3 us  [carried_state(): back = lax.all_to_all(before, axes, 0, 0, tiled=False)]
    dot_general x1 -> x0, local copies, waits for them, and re-layouts: 1.13 us -> none  [carried_state(): jnp.dot(earlier.astype(jnp.float32), gathered.reshape(devices, -1), preci...]
    unnamed x2 -> x0, local copies, waits for them, and re-layouts: 0.83 us -> none
  transfers between devices with their start and end apart: 1 -> 1, of which waited for: 1 -> 1; matrix products, arithmetic and copies ran while one was open for 0% -> 0% of each run, Pallas kernels for 9% -> 10%
where the time goes in v10:
time: 78.3 us; the launch traced here: 78 us
  blocking collectives  26.3 us (34%)
  Pallas kernels  22.6 us (29%)
  starting transfers between devices  15.6 us (20%)
  waiting for transfers between devices  12.5 us (16%)
    all_to_all x1, blocking collectives, carried_state(): back = lax.all_to_all(before, axes, 0, 0, tiled=False)  26.3 us
    all_to_all x1, starting transfers between devices, carried_state(): gathered = lax.all_to_all(pieces, axes, 0, 0, tiled=False)  15.6 us
    all_to_all x1, waiting for transfers between devices, carried_state(): gathered = lax.all_to_all(pieces, axes, 0, 0, tiled=False)  12.5 us
    pallas_call x1, Pallas kernels, layer(): pl.pallas_call(layer_kernel, out_shape=jax.ShapeDtypeStruct((rows, out_wi...  11.6 us
    pallas_call x1, Pallas kernels, intra_block(): pl.pallas_call(intra_kernel, out_shape=(jax.ShapeDtypeStruct((rows, width...  7.46 us
    pallas_call x1, Pallas kernels, state_totals(): pl.pallas_call(state_kernel, out_shape=jax.ShapeDtypeStruct((H, DH, DH),...  3.49 us
  transfers between devices with their start and end apart: 1, of which 1 were waited for; matrix products, arithmetic and copies ran while one was open for 0% of the time, Pallas kernels for 10%

profile of v10, /device:TPU:1, one launch (start us, length us, event | category | flops | bytes accessed | tf_op | source)
XLA Modules:
  0.0 78.0 jit_solution(13523601924347360460)
XLA Ops:
  0.0 3.5 %shard_map.55 = f32[8,128,128]{2,1,0:T(8,128)} custom-call(bf16[1024,1024]{1,0:T(8,128)(2,1)} %k_ref.3, bf16[1024,1024]{1,0:T(8,128)(2,1)} %v_ref.3), custom_call_target="tpu_custom_call" | custom-call | tf_op jit(solution)/shard_map/pallas_call | solution.py:57
  3.5 15.6 %all-to-all-start = ((f32[256,4,128]{2,1,0:T(4,128)}), f32[256,4,128]{2,1,0:T(4,128)S(1)}, u32[]{:S(2)}, u32[]{:S(2)}) async-start(f32[256,4,128]{2,1,0:T(4,128)} %bitcast.13), calls=%async_computation | async-start | bytes 1048576 | tf_op jit(solution)/shard_map/all_to_all | solution.py:23
  19.1 7.5 %shard_map.56 = (f32[1024,1024]{1,0:T(8,128)}, f32[8,8,128,128]{3,2,1,0:T(8,128)}) custom-call(bf16[1024,1024]{1,0:T(8,128)(2,1)} %q_ref.3, bf16[1024,1024]{1,0:T(8,128)(2,1)} %k_ref.3, bf16[1024,1024]{1,0:T(8,128)(2,1)} %v_ref.3), custom_call_target="tpu_custom_call" | custom-call | tf_op jit(solution)/shard_map/pallas_call | solution.py:105
  26.6 12.5 %all-to-all-done = f32[256,4,128]{2,1,0:T(4,128)S(1)} async-done(((f32[256,4,128]{2,1,0:T(4,128)}), f32[256,4,128]{2,1,0:T(4,128)S(1)}, u32[]{:S(2)}, u32[]{:S(2)}) %all-to-all-start) | async-done | bytes 524320 | tf_op jit(solution)/shard_map/all_to_all | solution.py:23
  39.1 0.2 copy.10
  39.3 0.4 fusion
  39.8 0.3 copy.9
  40.1 26.3 %all_to_all.10 = f32[256,4,128]{2,1,0:T(4,128)} all-to-all(f32[256,4,128]{2,1,0:T(4,128)S(1)} %copy.9), channel_id=1, replica_groups=mesh['outer'=32,'inner'=8] {'outer','inner'}, dimensions={0} | all-to-all | bytes 1048576 | tf_op jit(solution)/shard_map/all_to_all | solution.py:32
  66.4 11.6 %shard_map.57 = bf16[1024,2048]{1,0:T(8,128)(2,1)} custom-call(bf16[1024,1024]{1,0:T(8,128)(2,1)} %q_ref.3, f32[1024,1024]{1,0:T(8,128)} %get-tuple-element.12.i_ref, f32[8,8,128,128]{3,2,1,0:T(8,128)} %get-tuple-element.13.w_in_ref, f32[8,128,128]{2,1,0:T(8,128)} %bitcast.14, f32[1,1024]{1,0:T(1,128)} %bitcast.15, bf16[1024,2048]{1,0:T(8,128)(2,1)} %w_ref.1), custom_call_target="tpu_custom_call" | custom-call | tf_op jit(solution)/shard_map/pallas_call | solution.py:143
Async XLA Ops:
  3.5 35.6 %all-to-all-start = ((f32[256,4,128]{2,1,0:T(4,128)}), f32[256,4,128]{2,1,0:T(4,128)S(1)}, u32[]{:S(2)}, u32[]{:S(2)}) async-start(f32[256,4,128]{2,1,0:T(4,128)} %bitcast.13), calls=%async_computation | async-start | bytes 1048576 | tf_op jit(solution)/shard_map/all_to_all | solution.py:23
